TPU v7x, 768 devices: a whole 4x8x12 slice. The times are simulated.
768 devices in a mesh: face: 96 (over z_lo, y, core), tile: 8 (over x, z_hi).
Axes of the slice: x: 4, y: 8, z: 12 (z_hi: 2, z_lo: 6; z = z_hi * 6 + z_lo), core: 2. Of those that a mesh axis runs over, the one named last changes fastest.
Arguments:
- state: float32 [768, 4, 2, 128, 128], P(('face', 'tile')), may hold values from -3 to 3
- forcing: float32 [768, 2, 4, 128, 128], P(('face', 'tile')), may hold values from -3 to 3
- cotangent: float32 [768, 4, 2, 128, 128], P(('face', 'tile')), may hold values from -6 to 6
- neighbour: int32 [768, 4], P(('face', 'tile')), may hold values from -1 to 767, as said below
- rotation: int32 [768, 4], P(('face', 'tile')), may hold values from 0 to 7
- wet: int32 [768], P(('face', 'tile')), may hold values from 0 to 1, as said below
- levels: int32 [768, 128, 128], P(('face', 'tile')), may hold values from 0 to 2
Outputs:
- state_gradient: float32 [768, 4, 2, 128, 128], P(('face', 'tile'))
- forcing_gradient: float32 [768, 2, 4, 128, 128], P(('face', 'tile'))
Inputs may be any that keep to these rules, and one draw needn't show every extreme that they name: The west neighbour of every tile is the tile of the same slot on the device with the same tile index at face index one below (wrapping around the face axis), the east neighbour the one at face index one above; south and north neighbours lie on a device of the same face block or are -1. Every tile on a device of tile index 0 is wet.
All inputs are finite; a program needn't handle non-finite values.
Results may differ from a plain program's by a relative error of at most 0.00005.
Values sent between devices are 32-bit elements; how exact they have to be, the bound alone decides.
No kernel may reach another device: no remote copies, remote signals or barrier semaphores. Data moves between devices by JAX's collectives and lax.ppermute only.
A program may use at most 32 MiB of HBM per device.

v0:
```python
import jax
import jax.numpy as jnp
from jax import lax
from jax.sharding import PartitionSpec as P

time_step = 1.0
diffuse_rate = 0.15
viscosity = 0.15
vertical_mix = 0.1
coriolis = 0.3
buoyancy_scale = 0.25
thermal_coef = 1.0
haline_coef = 0.8
drag_rate = 0.05


def with_halo(block, sides, width):
    for axis, dim in sides:
        count = lax.axis_size(axis)
        forward = [(i, i + 1) for i in range(count - 1)]
        forward.append((count - 1, 0))
        backward = [(target, source) for source, target in forward]
        low = lax.ppermute(
            lax.slice_in_dim(block, block.shape[dim] - width, None, axis=dim), axis, forward
        )
        high = lax.ppermute(lax.slice_in_dim(block, 0, width, axis=dim), axis, backward)
        block = jnp.concatenate([low, block, high], axis=dim)
    return block


def edge_strips(field):
    return jnp.stack(
        [field[..., :, 0], field[..., :, -1], field[..., 0, :], field[..., -1, :]], axis=1
    )


def level_mix(values):
    above = jnp.concatenate([values[:, :1], values[:, :-1]], axis=1)
    below = jnp.concatenate([values[:, 1:], values[:, -1:]], axis=1)
    return above + below - 2.0 * values


def step_tiles(centre, halos, mask, drive):
    east = jnp.concatenate([centre[..., :, 1:], halos[:, 1][..., :, None]], axis=-1)
    west = jnp.concatenate([halos[:, 0][..., :, None], centre[..., :, :-1]], axis=-1)
    north = jnp.concatenate([centre[..., 1:, :], halos[:, 3][..., None, :]], axis=-2)
    south = jnp.concatenate([halos[:, 2][..., None, :], centre[..., :-1, :]], axis=-2)
    laplace = east + west + north + south - 4.0 * centre
    grad_x = 0.5 * (east - west)
    grad_y = 0.5 * (north - south)
    theta = centre[:, 0]
    salt = centre[:, 1]
    uvel = centre[:, 2]
    vvel = centre[:, 3]
    dens_x = -thermal_coef * grad_x[:, 0] + haline_coef * grad_x[:, 1]
    dens_y = -thermal_coef * grad_y[:, 0] + haline_coef * grad_y[:, 1]
    new_theta = theta + time_step * (
        -(uvel * grad_x[:, 0] + vvel * grad_y[:, 0])
        + diffuse_rate * laplace[:, 0]
        + vertical_mix * level_mix(theta)
    )
    new_salt = salt + time_step * (
        -(uvel * grad_x[:, 1] + vvel * grad_y[:, 1])
        + diffuse_rate * laplace[:, 1]
        + vertical_mix * level_mix(salt)
    )
    new_u = uvel + time_step * (
        viscosity * laplace[:, 2] + coriolis * vvel - buoyancy_scale * dens_x - drag_rate * uvel
    )
    new_v = vvel + time_step * (
        viscosity * laplace[:, 3] - coriolis * uvel - buoyancy_scale * dens_y - drag_rate * vvel
    )
    result = jnp.stack([new_theta, new_salt, new_u, new_v], axis=1)
    surface = result[:, :, 0:1] + (time_step * drive)[:, :, None]
    result = jnp.concatenate([surface, result[:, :, 1:]], axis=2)
    return result * mask[:, None]


def shards(state, forcing, cotangent, neighbour, rotation, wet, levels):
    slot_count = state.shape[0]
    group_size = lax.axis_size("tile")
    face_count = lax.axis_size("face")
    face_index = lax.axis_index("face")
    depth = jnp.arange(state.shape[2], dtype=jnp.int32)[None, :, None, None]
    mask = ((depth < levels[:, None]) & (wet[:, None, None, None] == 1)).astype(jnp.float32)
    valid = neighbour >= 0
    source = jnp.maximum(neighbour, 0)
    device_of = source // slot_count
    slot_of = source % slot_count
    source_face = device_of // group_size
    source_tile = device_of % group_size
    side = rotation % 4
    flip = rotation // 4
    lower_face = (face_index + face_count - 1) % face_count
    block = jnp.where(
        source_face == face_index,
        source_tile,
        jnp.where(source_face == lower_face, group_size, group_size + 1),
    )
    column = (block * slot_count + slot_of) * 4 + side
    total = (group_size + 2) * slot_count * 4
    selector = (
        (column[..., None] == jnp.arange(total, dtype=jnp.int32)) & valid[..., None]
    ).astype(jnp.float32)
    selector = selector.reshape(slot_count * 4, total)
    reverse = (flip == 1)[..., None, None, None]

    def gather_rims(field):
        strips = edge_strips(field)[None]
        copies = jnp.broadcast_to(strips, (group_size,) + strips.shape[1:])
        grouped = lax.all_to_all(copies, "tile", 0, 0, tiled=True)
        beside_all = with_halo(strips, (("face", 0),), 1)
        return jnp.concatenate([grouped, beside_all[0:1], beside_all[2:3]], axis=0)

    def assemble(field, candidates):
        flat = candidates.reshape(total, -1)
        chosen = jnp.dot(selector, flat, precision=lax.Precision.HIGHEST)
        chosen = chosen.reshape(slot_count, 4, field.shape[1], field.shape[2], field.shape[3])
        return jnp.where(reverse, chosen[..., ::-1], chosen)

    def fill(field):
        return assemble(field, gather_rims(field))

    def fill_back(ct_halos, field):
        cand_shape = (group_size + 2, slot_count, 4, field.shape[1], field.shape[2], field.shape[3])
        blank_cands = jnp.zeros(cand_shape, jnp.float32)
        unused, pull_assemble = jax.vjp(lambda c: assemble(field, c), blank_cands)
        (ct_cands,) = pull_assemble(ct_halos)
        returned = lax.all_to_all(ct_cands[:group_size], "tile", 0, 0, tiled=True)
        back_group = jnp.sum(returned, axis=0, keepdims=True)
        back_face = with_halo(ct_cands[group_size:], (("face", 0),), 1)
        ct_strips = back_group[0] + back_face[0] + back_face[3]
        unused_edges, pull_edges = jax.vjp(edge_strips, jnp.zeros_like(field))
        (extra,) = pull_edges(ct_strips)
        return extra

    def stepper(field, halos, drive):
        return step_tiles(field, halos, mask, drive)

    first = state * mask[:, None]
    halos_first = fill(first)
    second = step_tiles(first, halos_first, mask, forcing[:, 0])
    halos_second = fill(second)
    unused_a, pull_second = jax.vjp(stepper, second, halos_second, forcing[:, 1])
    ct_local_second, ct_halo_second, ct_drive_second = pull_second(cotangent)
    ct_second = ct_local_second + fill_back(ct_halo_second, second)
    unused_b, pull_first = jax.vjp(stepper, first, halos_first, forcing[:, 0])
    ct_local_first, ct_halo_first, ct_drive_first = pull_first(ct_second)
    ct_first = ct_local_first + fill_back(ct_halo_first, first)
    state_gradient = ct_first * mask[:, None]
    forcing_gradient = jnp.stack([ct_drive_first, ct_drive_second], axis=1)
    return (state_gradient, forcing_gradient)


def solution(mesh):
    placed = (
        P(("face", "tile"), None, None, None, None),
        P(("face", "tile"), None, None, None, None),
        P(("face", "tile"), None, None, None, None),
        P(("face", "tile"), None),
        P(("face", "tile"), None),
        P(("face", "tile")),
        P(("face", "tile"), None, None),
    )
    return jax.shard_map(
        shards,
        mesh=mesh,
        in_specs=placed,
        out_specs=(
            P(("face", "tile"), None, None, None, None),
            P(("face", "tile"), None, None, None, None),
        ),
        check_vma=False,
    )
```

profile of v0, /device:TPU:2, one launch (start us, length us, event | category | flops | bytes accessed | tf_op | source)
XLA Modules:
  0.0 187.2 jit_solution(13299230783146124142)
XLA Ops:
  2.3 1.3 copy.1155
  4.7 1.9 %collective-permute-start = (f32[1,1,4,4,2,128]{5,4,3,2,1,0:T(2,128)S(1)}, f32[1,1,4,4,2,128]{5,4,3,2,1,0:T(2,128)S(1)}, u32[]{:S(2)}, u32[]{:S(2)}) collective-permute-start(f32[1,1,4,4,2,128]{5,4,3,2,1,0:T(2,128)S(1)} %get-tuple-element.145), channel_id=1, source_target_pairs={{0,8},{8,16},{16,24},{24,32},{32,40},{40,48},{48,56},{56,64},{64,7... | collective-permute-start | bytes 49160 | tf_op jit(solution)/shard_map/ppermute | solution.py:23
  6.6 15.1 %collective-permute-start.1 = (f32[1,1,4,4,2,128]{5,4,3,2,1,0:T(2,128)S(1)}, f32[1,1,4,4,2,128]{5,4,3,2,1,0:T(2,128)S(1)}, u32[]{:S(2)}, u32[]{:S(2)}) collective-permute-start(f32[1,1,4,4,2,128]{5,4,3,2,1,0:T(2,128)S(1)} %get-tuple-element.145), channel_id=1, source_target_pairs={{8,0},{16,8},{24,16},{32,24},{40,32},{48,40},{56,48},{64,56},{72,6... | collective-permute-start | bytes 49160 | tf_op jit(solution)/shard_map/ppermute | solution.py:26
  22.3 13.0 %all-to-all-start = ((f32[8,1,4,4,2,128]{5,4,3,2,1,0:T(2,128)}), f32[8,1,4,4,2,128]{5,4,3,2,1,0:T(2,128)S(1)}, u32[]{:S(2)}, u32[]{:S(2)}) async-start(f32[8,1,4,4,2,128]{5,4,3,2,1,0:T(2,128)} %broadcast_in_dim.79), calls=%async_computation | async-start | bytes 262144 | tf_op jit(solution)/shard_map/all_to_all | solution.py:111
  35.3 1.5 fusion.69
  36.9 1.2 fusion.70
  41.6 5.1 %all-to-all-done = f32[8,1,4,4,2,128]{5,4,3,2,1,0:T(2,128)S(1)} async-done(((f32[8,1,4,4,2,128]{5,4,3,2,1,0:T(2,128)}), f32[8,1,4,4,2,128]{5,4,3,2,1,0:T(2,128)S(1)}, u32[]{:S(2)}, u32[]{:S(2)}) %all-to-all-start) | async-done | bytes 131104 | tf_op jit(solution)/shard_map/all_to_all | solution.py:111
  48.1 3.2 %subtract_multiply_fusion = (f32[1,4,2,128,128]{3,2,4,1,0:T(2,128)S(1)}, f32[1,4,2,128,128]{3,2,4,1,0:T(2,128)S(1)}, f32[1,4,2,128,128]{3,2,4,1,0:T(2,128)S(1)}) fusion(f32[1,4,2,127,128]{3,2,4,1,0:T(2,128)} %get-tuple-element.85, f32[1,4,2,1,128]{3,2,4,1,0:T(2,128)S(1)} %copy.1165, f32[1,4,2,1,128]{3,2,4,1,0:T(2,128)S(1)} %copy.1164, ...), kind=kLoop, calls=%fused_computation.47 | loop fusion | flops 1835008 | bytes 4325376 | tf_op jit(solution)/shard_map/mul | solution.py:50
  59.0 1.9 %collective-permute-start.2 = (f32[1,1,4,4,2,128]{5,4,3,2,1,0:T(2,128)}, f32[1,1,4,4,2,128]{5,4,3,2,1,0:T(2,128)}, u32[]{:S(2)}, u32[]{:S(2)}) collective-permute-start(f32[1,1,4,4,2,128]{5,4,3,2,1,0:T(2,128)} %get-tuple-element.139), channel_id=1, source_target_pairs={{0,8},{8,16},{16,24},{24,32},{32,40},{40,48},{48,56},{56,64},{64,7... | collective-permute-start | bytes 49160 | tf_op jit(solution)/shard_map/ppermute | solution.py:23
  60.9 10.6 %collective-permute-start.3 = (f32[1,1,4,4,2,128]{5,4,3,2,1,0:T(2,128)}, f32[1,1,4,4,2,128]{5,4,3,2,1,0:T(2,128)}, u32[]{:S(2)}, u32[]{:S(2)}) collective-permute-start(f32[1,1,4,4,2,128]{5,4,3,2,1,0:T(2,128)} %get-tuple-element.139), channel_id=1, source_target_pairs={{8,0},{16,8},{24,16},{32,24},{40,32},{48,40},{56,48},{64,56},{72,6... | collective-permute-start | bytes 49160 | tf_op jit(solution)/shard_map/ppermute | solution.py:26
  77.8 6.9 %all-to-all-start.1 = ((f32[8,1,4,4,2,128]{5,4,3,2,1,0:T(2,128)}), f32[8,1,4,4,2,128]{5,4,3,2,1,0:T(2,128)}, u32[]{:S(2)}, u32[]{:S(2)}) async-start(f32[8,1,4,4,2,128]{5,4,3,2,1,0:T(2,128)} %broadcast_in_dim.144), calls=%async_computation.1 | async-start | bytes 262144 | tf_op jit(solution)/shard_map/all_to_all | solution.py:111
  86.5 1.6 copy.1212
  88.1 1.7 fusion.64
  102.8 1.5 negate_multiply_fusion.9
  106.4 1.3 copy_multiply_fusion.1
  109.8 2.0 %copy_add_fusion.5 = (f32[1,4,2,128,128]{4,3,1,2,0:T(8,128)}, f32[1,4,2,128,128]{4,3,1,2,0:T(8,128)S(1)}) fusion(f32[1,4,2,128,128]{4,3,1,2,0:T(8,128)} %copy.1208, f32[1,4,2,128,128]{4,3,2,1,0:T(8,128)S(1)} %get-tuple-element.27, f32[1,1,2,128,128]{4,3,1,2,0:T(8,128)} %copy-done.13, f32[1,1,2,128,128]{4,3,1,2,0:T(8,128)S(1)} %copy.1296, ...), kind=kLoop, calls=%fused_computation.49 | loop fusion | flops 917504 | bytes 2621440 | tf_op jit(solution)/shard_map/transpose(jvp())/add_any | solution.py:48
  114.8 12.1 %all-to-all-start.2 = ((f32[8,1,4,4,2,128]{5,4,3,2,1,0:T(2,128)}), f32[8,1,4,4,2,128]{5,4,3,2,1,0:T(2,128)S(1)}, u32[]{:S(2)}, u32[]{:S(2)}) async-start(f32[8,1,4,4,2,128]{5,4,3,2,1,0:T(2,128)} %bitcast.54), calls=%async_computation.2 | async-start | bytes 262144 | tf_op jit(solution)/shard_map/all_to_all | solution.py:129
  127.0 2.1 %collective-permute-start.4 = (f32[1,1,4,4,2,128]{5,4,3,2,1,0:T(2,128)S(1)}, f32[1,1,4,4,2,128]{5,4,3,2,1,0:T(2,128)S(1)}, u32[]{:S(2)}, u32[]{:S(2)}) collective-permute-start(f32[1,1,4,4,2,128]{5,4,3,2,1,0:T(2,128)S(1)} %slice.271), channel_id=1, source_target_pairs={{0,8},{8,16},{16,24},{24,32},{32,40},{40,48},{48,56},{56,64},{64,7... | collective-permute-start | bytes 49160 | tf_op jit(solution)/shard_map/ppermute | solution.py:23
  129.1 10.8 %collective-permute-start.5 = (f32[1,1,4,4,2,128]{5,4,3,2,1,0:T(2,128)S(1)}, f32[1,1,4,4,2,128]{5,4,3,2,1,0:T(2,128)S(1)}, u32[]{:S(2)}, u32[]{:S(2)}) collective-permute-start(f32[1,1,4,4,2,128]{5,4,3,2,1,0:T(2,128)S(1)} %slice.273), channel_id=1, source_target_pairs={{8,0},{16,8},{24,16},{32,24},{40,32},{48,40},{56,48},{64,56},{72,6... | collective-permute-start | bytes 49160 | tf_op jit(solution)/shard_map/ppermute | solution.py:26
  143.2 1.4 fusion.7
  147.5 1.8 negate_multiply_fusion.7
  159.4 12.1 %all-to-all-start.3 = ((f32[8,1,4,4,2,128]{5,4,3,2,1,0:T(2,128)}), f32[8,1,4,4,2,128]{5,4,3,2,1,0:T(2,128)S(1)}, u32[]{:S(2)}, u32[]{:S(2)}) async-start(f32[8,1,4,4,2,128]{5,4,3,2,1,0:T(2,128)} %bitcast.72), calls=%async_computation.3 | async-start | bytes 262144 | tf_op jit(solution)/shard_map/all_to_all | solution.py:129
  171.6 1.9 %collective-permute-start.6 = (f32[1,1,4,4,2,128]{5,4,3,2,1,0:T(2,128)S(1)}, f32[1,1,4,4,2,128]{5,4,3,2,1,0:T(2,128)S(1)}, u32[]{:S(2)}, u32[]{:S(2)}) collective-permute-start(f32[1,1,4,4,2,128]{5,4,3,2,1,0:T(2,128)S(1)} %slice.277), channel_id=1, source_target_pairs={{0,8},{8,16},{16,24},{24,32},{32,40},{40,48},{48,56},{56,64},{64,7... | collective-permute-start | bytes 49160 | tf_op jit(solution)/shard_map/ppermute | solution.py:23
  173.6 10.6 %collective-permute-start.7 = (f32[1,1,4,4,2,128]{5,4,3,2,1,0:T(2,128)S(1)}, f32[1,1,4,4,2,128]{5,4,3,2,1,0:T(2,128)S(1)}, u32[]{:S(2)}, u32[]{:S(2)}) collective-permute-start(f32[1,1,4,4,2,128]{5,4,3,2,1,0:T(2,128)S(1)} %slice.279), channel_id=1, source_target_pairs={{8,0},{16,8},{24,16},{32,24},{40,32},{48,40},{56,48},{64,56},{72,6... | collective-permute-start | bytes 49160 | tf_op jit(solution)/shard_map/ppermute | solution.py:26
  (290 shorter events, 62.2 us)
Async XLA Ops:
  4.7 36.9 %collective-permute-start = (f32[1,1,4,4,2,128]{5,4,3,2,1,0:T(2,128)S(1)}, f32[1,1,4,4,2,128]{5,4,3,2,1,0:T(2,128)S(1)}, u32[]{:S(2)}, u32[]{:S(2)}) collective-permute-start(f32[1,1,4,4,2,128]{5,4,3,2,1,0:T(2,128)S(1)} %get-tuple-element.145), channel_id=1, source_target_pairs={{0,8},{8,16},{16,24},{24,32},{32,40},{40,48},{48,56},{56,64},{64,7... | collective-permute-start | bytes 49160 | tf_op jit(solution)/shard_map/ppermute | solution.py:23
  6.6 35.0 %collective-permute-start.1 = (f32[1,1,4,4,2,128]{5,4,3,2,1,0:T(2,128)S(1)}, f32[1,1,4,4,2,128]{5,4,3,2,1,0:T(2,128)S(1)}, u32[]{:S(2)}, u32[]{:S(2)}) collective-permute-start(f32[1,1,4,4,2,128]{5,4,3,2,1,0:T(2,128)S(1)} %get-tuple-element.145), channel_id=1, source_target_pairs={{8,0},{16,8},{24,16},{32,24},{40,32},{48,40},{56,48},{64,56},{72,6... | collective-permute-start | bytes 49160 | tf_op jit(solution)/shard_map/ppermute | solution.py:26
  22.3 24.4 %all-to-all-start = ((f32[8,1,4,4,2,128]{5,4,3,2,1,0:T(2,128)}), f32[8,1,4,4,2,128]{5,4,3,2,1,0:T(2,128)S(1)}, u32[]{:S(2)}, u32[]{:S(2)}) async-start(f32[8,1,4,4,2,128]{5,4,3,2,1,0:T(2,128)} %broadcast_in_dim.79), calls=%async_computation | async-start | bytes 262144 | tf_op jit(solution)/shard_map/all_to_all | solution.py:111
  39.6 7.5 %copy-start.44 = (pred[1,4,1,1,1,1,40]{6,1,5,4,3,2,0:T(4,128)(4,1)}, pred[1,4,1,1,1,1,40]{6,1,5,4,3,2,0:T(4,128)(4,1)S(1)}, u32[]{:S(2)}) copy-start(pred[1,4,1,1,1,1,40]{6,1,5,4,3,2,0:T(4,128)(4,1)S(1)} %fusion.49) | copy-start | bytes 484
  39.6 7.8 %copy-start.42 = (pred[4]{0:T(512)(128)(4,1)}, pred[4]{0:T(512)(128)(4,1)S(1)}, u32[]{:S(2)}) copy-start(pred[4]{0:T(512)(128)(4,1)S(1)} %compare_bitcast_fusion.1) | copy-start | bytes 16
  59.0 38.3 %collective-permute-start.2 = (f32[1,1,4,4,2,128]{5,4,3,2,1,0:T(2,128)}, f32[1,1,4,4,2,128]{5,4,3,2,1,0:T(2,128)}, u32[]{:S(2)}, u32[]{:S(2)}) collective-permute-start(f32[1,1,4,4,2,128]{5,4,3,2,1,0:T(2,128)} %get-tuple-element.139), channel_id=1, source_target_pairs={{0,8},{8,16},{16,24},{24,32},{32,40},{40,48},{48,56},{56,64},{64,7... | collective-permute-start | bytes 49160 | tf_op jit(solution)/shard_map/ppermute | solution.py:23
  60.9 36.4 %collective-permute-start.3 = (f32[1,1,4,4,2,128]{5,4,3,2,1,0:T(2,128)}, f32[1,1,4,4,2,128]{5,4,3,2,1,0:T(2,128)}, u32[]{:S(2)}, u32[]{:S(2)}) collective-permute-start(f32[1,1,4,4,2,128]{5,4,3,2,1,0:T(2,128)} %get-tuple-element.139), channel_id=1, source_target_pairs={{8,0},{16,8},{24,16},{32,24},{40,32},{48,40},{56,48},{64,56},{72,6... | collective-permute-start | bytes 49160 | tf_op jit(solution)/shard_map/ppermute | solution.py:26
  77.8 19.4 %all-to-all-start.1 = ((f32[8,1,4,4,2,128]{5,4,3,2,1,0:T(2,128)}), f32[8,1,4,4,2,128]{5,4,3,2,1,0:T(2,128)}, u32[]{:S(2)}, u32[]{:S(2)}) async-start(f32[8,1,4,4,2,128]{5,4,3,2,1,0:T(2,128)} %broadcast_in_dim.144), calls=%async_computation.1 | async-start | bytes 262144 | tf_op jit(solution)/shard_map/all_to_all | solution.py:111
  88.1 1.7 copy-start.33
  88.1 1.7 copy-start.34
  114.1 25.8 %copy-start.30 = (f32[1,1,2,128,128]{3,2,4,1,0:T(2,128)S(1)}, f32[1,1,2,128,128]{3,2,4,1,0:T(2,128)}, u32[]{:S(2)}) copy-start(f32[1,1,2,128,128]{3,2,4,1,0:T(2,128)} %get-tuple-element.149) | copy-start | bytes 393220
  114.8 25.1 %copy-start.21 = (f32[1,1,2,128,128]{3,2,4,1,0:T(2,128)S(1)}, f32[1,1,2,128,128]{3,2,4,1,0:T(2,128)}, u32[]{:S(2)}) copy-start(f32[1,1,2,128,128]{3,2,4,1,0:T(2,128)} %get-tuple-element.114) | copy-start | bytes 393220
  114.8 25.1 %copy-start.22 = (f32[1,1,2,128,128]{3,2,4,1,0:T(2,128)S(1)}, f32[1,1,2,128,128]{3,2,4,1,0:T(2,128)}, u32[]{:S(2)}) copy-start(f32[1,1,2,128,128]{3,2,4,1,0:T(2,128)} %get-tuple-element.115) | copy-start | bytes 393220
  114.8 27.0 %all-to-all-start.2 = ((f32[8,1,4,4,2,128]{5,4,3,2,1,0:T(2,128)}), f32[8,1,4,4,2,128]{5,4,3,2,1,0:T(2,128)S(1)}, u32[]{:S(2)}, u32[]{:S(2)}) async-start(f32[8,1,4,4,2,128]{5,4,3,2,1,0:T(2,128)} %bitcast.54), calls=%async_computation.2 | async-start | bytes 262144 | tf_op jit(solution)/shard_map/all_to_all | solution.py:129
  127.0 13.0 %copy-start.5 = (f32[1,4,2,127,128]{3,1,2,4,0:T(4,128)S(1)}, f32[1,4,2,127,128]{3,1,2,4,0:T(4,128)}, u32[]{:S(2)}) copy-start(f32[1,4,2,127,128]{3,1,2,4,0:T(4,128)} %split.125) | copy-start | bytes 1560580
  127.0 14.9 %collective-permute-start.4 = (f32[1,1,4,4,2,128]{5,4,3,2,1,0:T(2,128)S(1)}, f32[1,1,4,4,2,128]{5,4,3,2,1,0:T(2,128)S(1)}, u32[]{:S(2)}, u32[]{:S(2)}) collective-permute-start(f32[1,1,4,4,2,128]{5,4,3,2,1,0:T(2,128)S(1)} %slice.271), channel_id=1, source_target_pairs={{0,8},{8,16},{16,24},{24,32},{32,40},{40,48},{48,56},{56,64},{64,7... | collective-permute-start | bytes 49160 | tf_op jit(solution)/shard_map/ppermute | solution.py:23
  129.1 12.8 %collective-permute-start.5 = (f32[1,1,4,4,2,128]{5,4,3,2,1,0:T(2,128)S(1)}, f32[1,1,4,4,2,128]{5,4,3,2,1,0:T(2,128)S(1)}, u32[]{:S(2)}, u32[]{:S(2)}) collective-permute-start(f32[1,1,4,4,2,128]{5,4,3,2,1,0:T(2,128)S(1)} %slice.273), channel_id=1, source_target_pairs={{8,0},{16,8},{24,16},{32,24},{40,32},{48,40},{56,48},{64,56},{72,6... | collective-permute-start | bytes 49160 | tf_op jit(solution)/shard_map/ppermute | solution.py:26
  141.9 1.3 copy-start.4
  146.3 1.2 copy-start.3
  158.6 25.5 %copy-start.19 = (f32[1,1,4,128,128]{4,3,2,1,0:T(8,128)S(1)}, f32[1,1,4,128,128]{4,3,2,1,0:T(8,128)}, u32[]{:S(2)}) copy-start(f32[1,1,4,128,128]{4,3,2,1,0:T(8,128)} %get-tuple-element.43) | copy-start | bytes 786436
  159.4 24.7 %copy-start.18 = (f32[1,1,4,128,128]{4,3,2,1,0:T(8,128)S(1)}, f32[1,1,4,128,128]{4,3,2,1,0:T(8,128)}, u32[]{:S(2)}) copy-start(f32[1,1,4,128,128]{4,3,2,1,0:T(8,128)} %get-tuple-element.45) | copy-start | bytes 786436
  159.4 25.6 %all-to-all-start.3 = ((f32[8,1,4,4,2,128]{5,4,3,2,1,0:T(2,128)}), f32[8,1,4,4,2,128]{5,4,3,2,1,0:T(2,128)S(1)}, u32[]{:S(2)}, u32[]{:S(2)}) async-start(f32[8,1,4,4,2,128]{5,4,3,2,1,0:T(2,128)} %bitcast.72), calls=%async_computation.3 | async-start | bytes 262144 | tf_op jit(solution)/shard_map/all_to_all | solution.py:129
  171.6 13.4 %collective-permute-start.6 = (f32[1,1,4,4,2,128]{5,4,3,2,1,0:T(2,128)S(1)}, f32[1,1,4,4,2,128]{5,4,3,2,1,0:T(2,128)S(1)}, u32[]{:S(2)}, u32[]{:S(2)}) collective-permute-start(f32[1,1,4,4,2,128]{5,4,3,2,1,0:T(2,128)S(1)} %slice.277), channel_id=1, source_target_pairs={{0,8},{8,16},{16,24},{24,32},{32,40},{40,48},{48,56},{56,64},{64,7... | collective-permute-start | bytes 49160 | tf_op jit(solution)/shard_map/ppermute | solution.py:23
  173.6 12.0 %collective-permute-start.7 = (f32[1,1,4,4,2,128]{5,4,3,2,1,0:T(2,128)S(1)}, f32[1,1,4,4,2,128]{5,4,3,2,1,0:T(2,128)S(1)}, u32[]{:S(2)}, u32[]{:S(2)}) collective-permute-start(f32[1,1,4,4,2,128]{5,4,3,2,1,0:T(2,128)S(1)} %slice.279), channel_id=1, source_target_pairs={{8,0},{16,8},{24,16},{32,24},{40,32},{48,40},{56,48},{64,56},{72,6... | collective-permute-start | bytes 49160 | tf_op jit(solution)/shard_map/ppermute | solution.py:26
  (40 other events, 37.4 us)
where the time goes:
time: 189 us; the launch traced here: 187 us
  starting transfers between devices  98.9 us (52%)
  local copies, waits for them, and re-layouts  48.7 us (26%)
  other arithmetic  30.6 us (16%)
  waiting for transfers between devices  5.67 us (3%)
  between operations  2.47 us (1%)
    ppermute x4, starting transfers between devices, with_halo(): lax.ppermute(lax.slice_in_dim(block, 0, width, axis=dim), axis, backward)  47 us
    all_to_all x2, starting transfers between devices, fill_back(): returned = lax.all_to_all(ct_cands[:group_size], 'tile', 0, 0, tiled=True)  24.3 us
    unnamed x120, local copies, waits for them, and re-layouts  21.1 us
    all_to_all x2, starting transfers between devices, gather_rims(): grouped = lax.all_to_all(copies, 'tile', 0, 0, tiled=True)  19.9 us
    ppermute x4, starting transfers between devices, with_halo(): lax.ppermute(lax.slice_in_dim(block, block.shape[dim] - width, None, axis...  7.8 us
    mul x3, other arithmetic, step_tiles(): grad_y = 0.5 * (north - south)  5.63 us
    all_to_all x2, waiting for transfers between devices, gather_rims(): grouped = lax.all_to_all(copies, 'tile', 0, 0, tiled=True)  5.13 us
  transfers between devices with their start and end apart: 12, of which 2 were waited for; matrix products, arithmetic and copies ran while one was open for 12% of the time, Pallas kernels for 0%

commit v1 on v0

--- a/solution.py
+++ b/solution.py
@@ -40,11 +40,28 @@
     return above + below - 2.0 * values
 
 
+def shifted(centre, halo, axis, forward):
+    size = centre.shape[axis]
+    lead = [(0, 0)] * (centre.ndim - 2)
+    if axis == -1:
+        inner = centre[..., :, 1:] if forward else centre[..., :, :-1]
+        widths = lead + [(0, 0), (0, 1) if forward else (1, 0)]
+        spot = lax.broadcasted_iota(jnp.int32, centre.shape, centre.ndim - 1)
+        edge = halo[..., :, None]
+    else:
+        inner = centre[..., 1:, :] if forward else centre[..., :-1, :]
+        widths = lead + [(0, 1) if forward else (1, 0), (0, 0)]
+        spot = lax.broadcasted_iota(jnp.int32, centre.shape, centre.ndim - 2)
+        edge = halo[..., None, :]
+    at_edge = spot == (size - 1 if forward else 0)
+    return jnp.where(at_edge, edge, jnp.pad(inner, widths))
+
+
 def step_tiles(centre, halos, mask, drive):
-    east = jnp.concatenate([centre[..., :, 1:], halos[:, 1][..., :, None]], axis=-1)
-    west = jnp.concatenate([halos[:, 0][..., :, None], centre[..., :, :-1]], axis=-1)
-    north = jnp.concatenate([centre[..., 1:, :], halos[:, 3][..., None, :]], axis=-2)
-    south = jnp.concatenate([halos[:, 2][..., None, :], centre[..., :-1, :]], axis=-2)
+    east = shifted(centre, halos[:, 1], -1, True)
+    west = shifted(centre, halos[:, 0], -1, False)
+    north = shifted(centre, halos[:, 3], -2, True)
+    south = shifted(centre, halos[:, 2], -2, False)
     laplace = east + west + north + south - 4.0 * centre
     grad_x = 0.5 * (east - west)
     grad_y = 0.5 * (north - south)

time: 189 us -> 191 us (1.011)
  waiting for transfers between devices: 5.67 us -> 30.4 us
  starting transfers between devices: 98.9 us -> 78.3 us
  local copies, waits for them, and re-layouts: 48.7 us -> 42.8 us
  other arithmetic: 30.6 us -> 33.2 us
    ppermute x4, starting transfers between devices: 47 us -> 33.9 us  [with_halo(): lax.ppermute(lax.slice_in_dim(block, 0, width, axis=dim), axis, backward)]
    all_to_all x2, waiting for transfers between devices: 5.13 us -> 16.5 us  [gather_rims(): grouped = lax.all_to_all(copies, 'tile', 0, 0, tiled=True)]
    ppermute x4, waiting for transfers between devices: 0.01 us -> 10.1 us  [with_halo(): lax.ppermute(lax.slice_in_dim(block, block.shape[dim] - width, None, axis...]
    select_n x0 -> x8, other arithmetic: none -> 6.82 us  [shifted(): return jnp.where(at_edge, edge, jnp.pad(inner, widths))]
    all_to_all x2, starting transfers between devices: 24.3 us -> 18.2 us  [fill_back(): returned = lax.all_to_all(ct_cands[:group_size], 'tile', 0, 0, tiled=True)]
    unnamed x120 -> x88, local copies, waits for them, and re-layouts: 21.1 us -> 15 us
    mul x3 -> x2, other arithmetic: 5.63 us -> 0.23 us  [step_tiles(): grad_y = 0.5 * (north - south)]
    split x13 -> x0, local copies, waits for them, and re-layouts: 5.08 us -> none  [the longest x4 1.91 us: step_tiles(): jnp.concatenate([halos[:, 2][..., None, :], centre[..., :-1, :]], axis=-2)]
  transfers between devices with their start and end apart: 12 -> 12, of which waited for: 2 -> 5; matrix products, arithmetic and copies ran while one was open for 12% -> 8% of each run, Pallas kernels for 0% -> 0%
where the time goes in v1:
time: 191 us; the launch traced here: 189 us
  starting transfers between devices  78.3 us (41%)
  local copies, waits for them, and re-layouts  42.8 us (22%)
  other arithmetic  33.2 us (17%)
  waiting for transfers between devices  30.4 us (16%)
  matrix products  2.54 us (1%)
  between operations  2.03 us (1%)
    ppermute x4, starting transfers between devices, with_halo(): lax.ppermute(lax.slice_in_dim(block, 0, width, axis=dim), axis, backward)  33.9 us
    all_to_all x2, starting transfers between devices, fill_back(): returned = lax.all_to_all(ct_cands[:group_size], 'tile', 0, 0, tiled=True)  18.2 us
    all_to_all x2, starting transfers between devices, gather_rims(): grouped = lax.all_to_all(copies, 'tile', 0, 0, tiled=True)  18 us
    all_to_all x2, waiting for transfers between devices, gather_rims(): grouped = lax.all_to_all(copies, 'tile', 0, 0, tiled=True)  16.5 us
    unnamed x88, local copies, waits for them, and re-layouts  15 us
    ppermute x4, waiting for transfers between devices, with_halo(): lax.ppermute(lax.slice_in_dim(block, block.shape[dim] - width, None, axis...  10.1 us
    ppermute x4, starting transfers between devices, with_halo(): lax.ppermute(lax.slice_in_dim(block, block.shape[dim] - width, None, axis...  8.17 us
    select_n x8, other arithmetic, shifted(): return jnp.where(at_edge, edge, jnp.pad(inner, widths))  6.82 us
  transfers between devices with their start and end apart: 12, of which 5 were waited for; matrix products, arithmetic and copies ran while one was open for 8% of the time, Pallas kernels for 0%

profile of v1, /device:TPU:2, one launch (start us, length us, event | category | flops | bytes accessed | tf_op | source)
XLA Modules:
  0.0 189.3 jit_solution(15749144686156729711)
XLA Ops:
  3.9 15.1 %collective-permute-start.1 = (f32[1,1,4,4,2,128]{5,4,3,2,1,0:T(2,128)S(1)}, f32[1,1,4,4,2,128]{5,4,3,2,1,0:T(2,128)S(1)}, u32[]{:S(2)}, u32[]{:S(2)}) collective-permute-start(f32[1,1,4,4,2,128]{5,4,3,2,1,0:T(2,128)S(1)} %get-tuple-element.144), channel_id=1, source_target_pairs={{8,0},{16,8},{24,16},{32,24},{40,32},{48,40},{56,48},{64,56},{72,6... | collective-permute-start | bytes 49160 | tf_op jit(solution)/shard_map/ppermute | solution.py:26
  18.9 1.9 %collective-permute-start = (f32[1,1,4,4,2,128]{5,4,3,2,1,0:T(2,128)S(1)}, f32[1,1,4,4,2,128]{5,4,3,2,1,0:T(2,128)S(1)}, u32[]{:S(2)}, u32[]{:S(2)}) collective-permute-start(f32[1,1,4,4,2,128]{5,4,3,2,1,0:T(2,128)S(1)} %get-tuple-element.144), channel_id=1, source_target_pairs={{0,8},{8,16},{16,24},{24,32},{32,40},{40,48},{48,56},{56,64},{64,7... | collective-permute-start | bytes 49160 | tf_op jit(solution)/shard_map/ppermute | solution.py:23
  21.6 12.4 %all-to-all-start = ((f32[8,1,4,4,2,128]{5,4,3,2,1,0:T(2,128)}), f32[8,1,4,4,2,128]{5,4,3,2,1,0:T(2,128)S(1)}, u32[]{:S(2)}, u32[]{:S(2)}) async-start(f32[8,1,4,4,2,128]{5,4,3,2,1,0:T(2,128)} %broadcast_in_dim.241), calls=%async_computation | async-start | bytes 262144 | tf_op jit(solution)/shard_map/all_to_all | solution.py:128
  36.5 8.8 %all-to-all-done = f32[8,1,4,4,2,128]{5,4,3,2,1,0:T(2,128)S(1)} async-done(((f32[8,1,4,4,2,128]{5,4,3,2,1,0:T(2,128)}), f32[8,1,4,4,2,128]{5,4,3,2,1,0:T(2,128)S(1)}, u32[]{:S(2)}, u32[]{:S(2)}) %all-to-all-start) | async-done | bytes 131104 | tf_op jit(solution)/shard_map/all_to_all | solution.py:128
  54.6 8.5 %collective-permute-start.3 = (f32[1,1,4,4,2,128]{5,3,4,2,1,0:T(4,128)S(1)}, f32[1,1,4,4,2,128]{5,3,4,2,1,0:T(4,128)}, u32[]{:S(2)}, u32[]{:S(2)}) collective-permute-start(f32[1,1,4,4,2,128]{5,3,4,2,1,0:T(4,128)S(1)} %get-tuple-element.138), channel_id=1, source_target_pairs={{8,0},{16,8},{24,16},{32,24},{40,32},{48,40},{56,48},{64,56},{72,6... | collective-permute-start | bytes 49160 | tf_op jit(solution)/shard_map/ppermute | solution.py:26
  63.1 1.9 %collective-permute-start.2 = (f32[1,1,4,4,2,128]{5,3,4,2,1,0:T(4,128)S(1)}, f32[1,1,4,4,2,128]{5,3,4,2,1,0:T(4,128)}, u32[]{:S(2)}, u32[]{:S(2)}) collective-permute-start(f32[1,1,4,4,2,128]{5,3,4,2,1,0:T(4,128)S(1)} %get-tuple-element.138), channel_id=1, source_target_pairs={{0,8},{8,16},{16,24},{24,32},{32,40},{40,48},{48,56},{56,64},{64,7... | collective-permute-start | bytes 49160 | tf_op jit(solution)/shard_map/ppermute | solution.py:23
  68.1 5.6 %all-to-all-start.1 = ((f32[8,1,4,4,2,128]{5,4,3,2,1,0:T(2,128)}), f32[8,1,4,4,2,128]{5,4,3,2,1,0:T(2,128)S(1)}, u32[]{:S(2)}, u32[]{:S(2)}) async-start(f32[8,1,4,4,2,128]{5,4,3,2,1,0:T(2,128)} %broadcast_in_dim.252), calls=%async_computation.1 | async-start | bytes 262144 | tf_op jit(solution)/shard_map/all_to_all | solution.py:128
  77.4 7.7 %all-to-all-done.1 = f32[8,1,4,4,2,128]{5,4,3,2,1,0:T(2,128)S(1)} async-done(((f32[8,1,4,4,2,128]{5,4,3,2,1,0:T(2,128)}), f32[8,1,4,4,2,128]{5,4,3,2,1,0:T(2,128)S(1)}, u32[]{:S(2)}, u32[]{:S(2)}) %all-to-all-start.1) | async-done | bytes 131104 | tf_op jit(solution)/shard_map/all_to_all | solution.py:128
  85.9 1.8 reshape.917
  87.6 1.7 dot_general.24
  106.5 2.1 %slice_select_fusion.4 = f32[1,4,2,128,127]{4,3,1,2,0:T(8,128)} fusion(f32[1,4,2,128,128]{4,3,1,2,0:T(8,128)} %get-tuple-element.73, pred[127]{0:T(512)(128)(4,1)S(1)} %copy-done.31), kind=kLoop, calls=%fused_computation.5 | loop fusion | flops 130048 | bytes 1040511 | tf_op jit(solution)/shard_map/transpose(jvp(jit(_where)))/select_n | solution.py:57
  112.6 5.5 %all-to-all-start.2 = ((f32[8,1,4,4,2,128]{5,4,3,2,1,0:T(2,128)}), f32[8,1,4,4,2,128]{5,4,3,2,1,0:T(2,128)}, u32[]{:S(2)}, u32[]{:S(2)}) async-start(f32[8,1,4,4,2,128]{5,4,3,2,1,0:T(2,128)} %bitcast.451), calls=%async_computation.2 | async-start | bytes 262144 | tf_op jit(solution)/shard_map/all_to_all | solution.py:146
  119.4 8.4 %collective-permute-start.5 = (f32[1,1,4,4,2,128]{5,4,3,2,1,0:T(2,128)}, f32[1,1,4,4,2,128]{5,4,3,2,1,0:T(2,128)}, u32[]{:S(2)}, u32[]{:S(2)}) collective-permute-start(f32[1,1,4,4,2,128]{5,4,3,2,1,0:T(2,128)} %slice.281), channel_id=1, source_target_pairs={{8,0},{16,8},{24,16},{32,24},{40,32},{48,40},{56,48},{64,56},{72,6... | collective-permute-start | bytes 49160 | tf_op jit(solution)/shard_map/ppermute | solution.py:26
  127.8 1.9 %collective-permute-start.4 = (f32[1,1,4,4,2,128]{5,4,3,2,1,0:T(2,128)}, f32[1,1,4,4,2,128]{5,4,3,2,1,0:T(2,128)}, u32[]{:S(2)}, u32[]{:S(2)}) collective-permute-start(f32[1,1,4,4,2,128]{5,4,3,2,1,0:T(2,128)} %slice.279), channel_id=1, source_target_pairs={{0,8},{8,16},{16,24},{24,32},{32,40},{40,48},{48,56},{56,64},{64,7... | collective-permute-start | bytes 49160 | tf_op jit(solution)/shard_map/ppermute | solution.py:23
  132.5 7.7 %collective-permute-done.4 = f32[1,1,4,4,2,128]{5,4,3,2,1,0:T(2,128)} collective-permute-done((f32[1,1,4,4,2,128]{5,4,3,2,1,0:T(2,128)}, f32[1,1,4,4,2,128]{5,4,3,2,1,0:T(2,128)}, u32[]{:S(2)}, u32[]{:S(2)}) %collective-permute-start.4) | collective-permute-done | bytes 16416 | tf_op jit(solution)/shard_map/ppermute | solution.py:23
  141.4 2.1 %fusion.11 = f32[1,4,2,128,128]{4,3,1,2,0:T(8,128)S(1)} fusion(f32[1,1,2,128,128]{4,3,1,2,0:T(8,128)} %get-tuple-element.46, f32[1,1,2,128,128]{4,3,1,2,0:T(8,128)} %get-tuple-element.45, f32[1,1,2,128,128]{4,3,1,2,0:T(8,128)} %get-tuple-element.85, f32[1,4,2,128,1]{4,3,1,2,0:T(8,128)S(1)} %copy.618, f32[1,4,2,128,1]{4,3,1,2,0:T(8,128)S(1)} %copy.616, ...), kind=kLoop, calls=%fused_computation.28 | loop fusion | flops 2228224 | bytes 3670016 | tf_op jit(solution)/shard_map/add | solution.py:163
  145.0 1.7 bitcast_add_fusion.2
  157.4 1.7 slice.283
  159.1 12.7 %all-to-all-start.3 = ((f32[8,1,4,4,2,128]{5,4,3,2,1,0:T(2,128)}), f32[8,1,4,4,2,128]{5,4,3,2,1,0:T(2,128)S(1)}, u32[]{:S(2)}, u32[]{:S(2)}) async-start(f32[8,1,4,4,2,128]{5,4,3,2,1,0:T(2,128)} %bitcast.107), calls=%async_computation.3 | async-start | bytes 262144 | tf_op jit(solution)/shard_map/all_to_all | solution.py:146
  171.8 1.9 %collective-permute-start.7 = (f32[1,1,4,4,2,128]{5,4,3,2,1,0:T(2,128)S(1)}, f32[1,1,4,4,2,128]{5,4,3,2,1,0:T(2,128)S(1)}, u32[]{:S(2)}, u32[]{:S(2)}) collective-permute-start(f32[1,1,4,4,2,128]{5,4,3,2,1,0:T(2,128)S(1)} %slice.287), channel_id=1, source_target_pairs={{8,0},{16,8},{24,16},{32,24},{40,32},{48,40},{56,48},{64,56},{72,6... | collective-permute-start | bytes 49160 | tf_op jit(solution)/shard_map/ppermute | solution.py:26
  173.7 2.4 %collective-permute-start.6 = (f32[1,1,4,4,2,128]{5,4,3,2,1,0:T(2,128)S(1)}, f32[1,1,4,4,2,128]{5,4,3,2,1,0:T(2,128)S(1)}, u32[]{:S(2)}, u32[]{:S(2)}) collective-permute-start(f32[1,1,4,4,2,128]{5,4,3,2,1,0:T(2,128)S(1)} %slice.285), channel_id=1, source_target_pairs={{0,8},{8,16},{16,24},{24,32},{32,40},{40,48},{48,56},{56,64},{64,7... | collective-permute-start | bytes 49160 | tf_op jit(solution)/shard_map/ppermute | solution.py:23
  179.5 3.7 %all-to-all-done.3 = f32[8,1,4,4,2,128]{5,4,3,2,1,0:T(2,128)S(1)} async-done(((f32[8,1,4,4,2,128]{5,4,3,2,1,0:T(2,128)}), f32[8,1,4,4,2,128]{5,4,3,2,1,0:T(2,128)S(1)}, u32[]{:S(2)}, u32[]{:S(2)}) %all-to-all-start.3) | async-done | bytes 131104 | tf_op jit(solution)/shard_map/all_to_all | solution.py:146
  183.2 2.5 %collective-permute-done.6 = f32[1,1,4,4,2,128]{5,4,3,2,1,0:T(2,128)S(1)} collective-permute-done((f32[1,1,4,4,2,128]{5,4,3,2,1,0:T(2,128)S(1)}, f32[1,1,4,4,2,128]{5,4,3,2,1,0:T(2,128)S(1)}, u32[]{:S(2)}, u32[]{:S(2)}) %collective-permute-start.6) | collective-permute-done | bytes 16416 | tf_op jit(solution)/shard_map/ppermute | solution.py:23
  186.9 2.3 %fusion.13 = f32[1,4,2,128,128]{4,3,2,1,0:T(8,128)} fusion(f32[1,4,2,128,1]{4,3,2,1,0:T(8,128)S(1)} %copy.669, f32[1,4,2,128,1]{4,3,2,1,0:T(8,128)S(1)} %copy.668, f32[1,4,2,1,128]{4,3,2,1,0:T(1,128)S(1)} %bitcast.482, f32[1,4,2,1,128]{4,3,2,1,0:T(1,128)S(1)} %bitcast.481, f32[1,4,2,128,127]{4,3,2,1,0:T(8,128)} %slice_select_fusion, ...), kind=kLoop, calls=%fused_computation.34 | loop fusion | flops 1966080 | bytes 3801088 | tf_op jit(solution)/shard_map/mul | solution.py:167
  (209 shorter events, 65.2 us)
Async XLA Ops:
  3.9 32.7 %collective-permute-start.1 = (f32[1,1,4,4,2,128]{5,4,3,2,1,0:T(2,128)S(1)}, f32[1,1,4,4,2,128]{5,4,3,2,1,0:T(2,128)S(1)}, u32[]{:S(2)}, u32[]{:S(2)}) collective-permute-start(f32[1,1,4,4,2,128]{5,4,3,2,1,0:T(2,128)S(1)} %get-tuple-element.144), channel_id=1, source_target_pairs={{8,0},{16,8},{24,16},{32,24},{40,32},{48,40},{56,48},{64,56},{72,6... | collective-permute-start | bytes 49160 | tf_op jit(solution)/shard_map/ppermute | solution.py:26
  18.9 17.6 %collective-permute-start = (f32[1,1,4,4,2,128]{5,4,3,2,1,0:T(2,128)S(1)}, f32[1,1,4,4,2,128]{5,4,3,2,1,0:T(2,128)S(1)}, u32[]{:S(2)}, u32[]{:S(2)}) collective-permute-start(f32[1,1,4,4,2,128]{5,4,3,2,1,0:T(2,128)S(1)} %get-tuple-element.144), channel_id=1, source_target_pairs={{0,8},{8,16},{16,24},{24,32},{32,40},{40,48},{48,56},{56,64},{64,7... | collective-permute-start | bytes 49160 | tf_op jit(solution)/shard_map/ppermute | solution.py:23
  21.6 23.8 %all-to-all-start = ((f32[8,1,4,4,2,128]{5,4,3,2,1,0:T(2,128)}), f32[8,1,4,4,2,128]{5,4,3,2,1,0:T(2,128)S(1)}, u32[]{:S(2)}, u32[]{:S(2)}) async-start(f32[8,1,4,4,2,128]{5,4,3,2,1,0:T(2,128)} %broadcast_in_dim.241), calls=%async_computation | async-start | bytes 262144 | tf_op jit(solution)/shard_map/all_to_all | solution.py:128
  35.8 9.9 %copy-start.33 = (pred[1,4,1,1,1,1,40]{6,1,5,4,3,2,0:T(4,128)(4,1)}, pred[1,4,1,1,1,1,40]{6,1,5,4,3,2,0:T(4,128)(4,1)S(1)}, u32[]{:S(2)}) copy-start(pred[1,4,1,1,1,1,40]{6,1,5,4,3,2,0:T(4,128)(4,1)S(1)} %fusion.94) | copy-start | bytes 484
  35.8 10.2 %copy-start.28 = (pred[4]{0:T(512)(128)(4,1)}, pred[4]{0:T(512)(128)(4,1)S(1)}, u32[]{:S(2)}) copy-start(pred[4]{0:T(512)(128)(4,1)S(1)} %compare_bitcast_fusion.1) | copy-start | bytes 16
  35.9 10.2 %copy-start.20 = (pred[128]{0:T(512)(128)(4,1)}, pred[128]{0:T(512)(128)(4,1)S(1)}, u32[]{:S(2)}) copy-start(pred[128]{0:T(512)(128)(4,1)S(1)} %get-tuple-element.146) | copy-start | bytes 388
  35.9 10.2 %copy-start.25 = (pred[128]{0:T(512)(128)(4,1)}, pred[128]{0:T(512)(128)(4,1)S(1)}, u32[]{:S(2)}) copy-start(pred[128]{0:T(512)(128)(4,1)S(1)} %get-tuple-element.145) | copy-start | bytes 388
  46.1 1.7 copy-start
  54.6 21.3 %collective-permute-start.3 = (f32[1,1,4,4,2,128]{5,3,4,2,1,0:T(4,128)S(1)}, f32[1,1,4,4,2,128]{5,3,4,2,1,0:T(4,128)}, u32[]{:S(2)}, u32[]{:S(2)}) collective-permute-start(f32[1,1,4,4,2,128]{5,3,4,2,1,0:T(4,128)S(1)} %get-tuple-element.138), channel_id=1, source_target_pairs={{8,0},{16,8},{24,16},{32,24},{40,32},{48,40},{56,48},{64,56},{72,6... | collective-permute-start | bytes 49160 | tf_op jit(solution)/shard_map/ppermute | solution.py:26
  63.1 13.5 %collective-permute-start.2 = (f32[1,1,4,4,2,128]{5,3,4,2,1,0:T(4,128)S(1)}, f32[1,1,4,4,2,128]{5,3,4,2,1,0:T(4,128)}, u32[]{:S(2)}, u32[]{:S(2)}) collective-permute-start(f32[1,1,4,4,2,128]{5,3,4,2,1,0:T(4,128)S(1)} %get-tuple-element.138), channel_id=1, source_target_pairs={{0,8},{8,16},{16,24},{24,32},{32,40},{40,48},{48,56},{56,64},{64,7... | collective-permute-start | bytes 49160 | tf_op jit(solution)/shard_map/ppermute | solution.py:23
  68.1 17.0 %all-to-all-start.1 = ((f32[8,1,4,4,2,128]{5,4,3,2,1,0:T(2,128)}), f32[8,1,4,4,2,128]{5,4,3,2,1,0:T(2,128)S(1)}, u32[]{:S(2)}, u32[]{:S(2)}) async-start(f32[8,1,4,4,2,128]{5,4,3,2,1,0:T(2,128)} %broadcast_in_dim.252), calls=%async_computation.1 | async-start | bytes 262144 | tf_op jit(solution)/shard_map/all_to_all | solution.py:128
  85.9 6.1 %copy-start.5 = (f32[1,4,2,128,127]{4,3,1,2,0:T(8,128)S(1)}, f32[1,4,2,128,127]{4,3,1,2,0:T(8,128)}, u32[]{:S(2)}) copy-start(f32[1,4,2,128,127]{4,3,1,2,0:T(8,128)} %get-tuple-element.70) | copy-start | bytes 1560580
  94.2 1.1 copy-start.3
  94.2 1.2 copy-start.4
  102.2 1.3 copy-start.34
  106.5 2.1 %copy-start.7 = (f32[1,4,2,128,128]{4,3,1,2,0:T(8,128)S(1)}, f32[1,4,2,128,128]{4,3,1,2,0:T(8,128)}, u32[]{:S(2)}) copy-start(f32[1,4,2,128,128]{4,3,1,2,0:T(8,128)} %get-tuple-element.75) | copy-start | bytes 1572868
  112.6 19.0 %all-to-all-start.2 = ((f32[8,1,4,4,2,128]{5,4,3,2,1,0:T(2,128)}), f32[8,1,4,4,2,128]{5,4,3,2,1,0:T(2,128)}, u32[]{:S(2)}, u32[]{:S(2)}) async-start(f32[8,1,4,4,2,128]{5,4,3,2,1,0:T(2,128)} %bitcast.451), calls=%async_computation.2 | async-start | bytes 262144 | tf_op jit(solution)/shard_map/all_to_all | solution.py:146
  119.4 13.1 %collective-permute-start.5 = (f32[1,1,4,4,2,128]{5,4,3,2,1,0:T(2,128)}, f32[1,1,4,4,2,128]{5,4,3,2,1,0:T(2,128)}, u32[]{:S(2)}, u32[]{:S(2)}) collective-permute-start(f32[1,1,4,4,2,128]{5,4,3,2,1,0:T(2,128)} %slice.281), channel_id=1, source_target_pairs={{8,0},{16,8},{24,16},{32,24},{40,32},{48,40},{56,48},{64,56},{72,6... | collective-permute-start | bytes 49160 | tf_op jit(solution)/shard_map/ppermute | solution.py:26
  127.8 12.3 %collective-permute-start.4 = (f32[1,1,4,4,2,128]{5,4,3,2,1,0:T(2,128)}, f32[1,1,4,4,2,128]{5,4,3,2,1,0:T(2,128)}, u32[]{:S(2)}, u32[]{:S(2)}) collective-permute-start(f32[1,1,4,4,2,128]{5,4,3,2,1,0:T(2,128)} %slice.279), channel_id=1, source_target_pairs={{0,8},{8,16},{16,24},{24,32},{32,40},{40,48},{48,56},{56,64},{64,7... | collective-permute-start | bytes 49160 | tf_op jit(solution)/shard_map/ppermute | solution.py:23
  157.4 1.7 copy-start.23
  159.1 12.7 %copy-start.22 = (f32[4,1024]{1,0:T(4,128)S(1)}, f32[4,1024]{1,0:T(4,128)}, u32[]{:S(2)}) copy-start(f32[4,1024]{1,0:T(4,128)} %get-tuple-element.109) | copy-start | bytes 49156
  159.1 24.0 %all-to-all-start.3 = ((f32[8,1,4,4,2,128]{5,4,3,2,1,0:T(2,128)}), f32[8,1,4,4,2,128]{5,4,3,2,1,0:T(2,128)S(1)}, u32[]{:S(2)}, u32[]{:S(2)}) async-start(f32[8,1,4,4,2,128]{5,4,3,2,1,0:T(2,128)} %bitcast.107), calls=%async_computation.3 | async-start | bytes 262144 | tf_op jit(solution)/shard_map/all_to_all | solution.py:146
  171.8 11.4 %collective-permute-start.7 = (f32[1,1,4,4,2,128]{5,4,3,2,1,0:T(2,128)S(1)}, f32[1,1,4,4,2,128]{5,4,3,2,1,0:T(2,128)S(1)}, u32[]{:S(2)}, u32[]{:S(2)}) collective-permute-start(f32[1,1,4,4,2,128]{5,4,3,2,1,0:T(2,128)S(1)} %slice.287), channel_id=1, source_target_pairs={{8,0},{16,8},{24,16},{32,24},{40,32},{48,40},{56,48},{64,56},{72,6... | collective-permute-start | bytes 49160 | tf_op jit(solution)/shard_map/ppermute | solution.py:26
  173.7 12.0 %collective-permute-start.6 = (f32[1,1,4,4,2,128]{5,4,3,2,1,0:T(2,128)S(1)}, f32[1,1,4,4,2,128]{5,4,3,2,1,0:T(2,128)S(1)}, u32[]{:S(2)}, u32[]{:S(2)}) collective-permute-start(f32[1,1,4,4,2,128]{5,4,3,2,1,0:T(2,128)S(1)} %slice.285), channel_id=1, source_target_pairs={{0,8},{8,16},{16,24},{24,32},{32,40},{40,48},{48,56},{56,64},{64,7... | collective-permute-start | bytes 49160 | tf_op jit(solution)/shard_map/ppermute | solution.py:23
  (30 other events, 24.9 us)

commit v2 on v0

--- a/solution.py
+++ b/solution.py
@@ -124,13 +124,13 @@
     def fill_back(ct_halos, field):
         cand_shape = (group_size + 2, slot_count, 4, field.shape[1], field.shape[2], field.shape[3])
         blank_cands = jnp.zeros(cand_shape, jnp.float32)
-        unused, pull_assemble = jax.vjp(lambda c: assemble(field, c), blank_cands)
+        _, pull_assemble = jax.vjp(lambda c: assemble(field, c), blank_cands)
         (ct_cands,) = pull_assemble(ct_halos)
         returned = lax.all_to_all(ct_cands[:group_size], "tile", 0, 0, tiled=True)
         back_group = jnp.sum(returned, axis=0, keepdims=True)
         back_face = with_halo(ct_cands[group_size:], (("face", 0),), 1)
         ct_strips = back_group[0] + back_face[0] + back_face[3]
-        unused_edges, pull_edges = jax.vjp(edge_strips, jnp.zeros_like(field))
+        _, pull_edges = jax.vjp(edge_strips, jnp.zeros_like(field))
         (extra,) = pull_edges(ct_strips)
         return extra
 
@@ -141,10 +141,10 @@
     halos_first = fill(first)
     second = step_tiles(first, halos_first, mask, forcing[:, 0])
     halos_second = fill(second)
-    unused_a, pull_second = jax.vjp(stepper, second, halos_second, forcing[:, 1])
+    _, pull_second = jax.vjp(stepper, second, halos_second, forcing[:, 1])
     ct_local_second, ct_halo_second, ct_drive_second = pull_second(cotangent)
     ct_second = ct_local_second + fill_back(ct_halo_second, second)
-    unused_b, pull_first = jax.vjp(stepper, first, halos_first, forcing[:, 0])
+    _, pull_first = jax.vjp(stepper, first, halos_first, forcing[:, 0])
     ct_local_first, ct_halo_first, ct_drive_first = pull_first(ct_second)
     ct_first = ct_local_first + fill_back(ct_halo_first, first)
     state_gradient = ct_first * mask[:, None]

time: 189 us -> 189 us (level)
  no operation moved by 1% of the time
where the time goes in v2:
time: 189 us; the launch traced here: 187 us
  starting transfers between devices  98.9 us (52%)
  local copies, waits for them, and re-layouts  48.7 us (26%)
  other arithmetic  30.6 us (16%)
  waiting for transfers between devices  5.67 us (3%)
  between operations  2.47 us (1%)
    ppermute x4, starting transfers between devices, with_halo(): lax.ppermute(lax.slice_in_dim(block, 0, width, axis=dim), axis, backward)  47 us
    all_to_all x2, starting transfers between devices, fill_back(): returned = lax.all_to_all(ct_cands[:group_size], 'tile', 0, 0, tiled=True)  24.3 us
    unnamed x120, local copies, waits for them, and re-layouts  21.1 us
    all_to_all x2, starting transfers between devices, gather_rims(): grouped = lax.all_to_all(copies, 'tile', 0, 0, tiled=True)  19.9 us
    ppermute x4, starting transfers between devices, with_halo(): lax.ppermute(lax.slice_in_dim(block, block.shape[dim] - width, None, axis...  7.8 us
    mul x3, other arithmetic, step_tiles(): grad_y = 0.5 * (north - south)  5.63 us
    all_to_all x2, waiting for transfers between devices, gather_rims(): grouped = lax.all_to_all(copies, 'tile', 0, 0, tiled=True)  5.13 us
  transfers between devices with their start and end apart: 12, of which 2 were waited for; matrix products, arithmetic and copies ran while one was open for 12% of the time, Pallas kernels for 0%

profile of v2, /device:TPU:2, one launch (start us, length us, event | category | flops | bytes accessed | tf_op | source)
XLA Modules:
  0.0 187.2 jit_solution(13299230783146124142)
XLA Ops:
  2.3 1.3 copy.1155
  4.7 1.9 %collective-permute-start = (f32[1,1,4,4,2,128]{5,4,3,2,1,0:T(2,128)S(1)}, f32[1,1,4,4,2,128]{5,4,3,2,1,0:T(2,128)S(1)}, u32[]{:S(2)}, u32[]{:S(2)}) collective-permute-start(f32[1,1,4,4,2,128]{5,4,3,2,1,0:T(2,128)S(1)} %get-tuple-element.145), channel_id=1, source_target_pairs={{0,8},{8,16},{16,24},{24,32},{32,40},{40,48},{48,56},{56,64},{64,7... | collective-permute-start | bytes 49160 | tf_op jit(solution)/shard_map/ppermute | solution.py:23
  6.6 15.1 %collective-permute-start.1 = (f32[1,1,4,4,2,128]{5,4,3,2,1,0:T(2,128)S(1)}, f32[1,1,4,4,2,128]{5,4,3,2,1,0:T(2,128)S(1)}, u32[]{:S(2)}, u32[]{:S(2)}) collective-permute-start(f32[1,1,4,4,2,128]{5,4,3,2,1,0:T(2,128)S(1)} %get-tuple-element.145), channel_id=1, source_target_pairs={{8,0},{16,8},{24,16},{32,24},{40,32},{48,40},{56,48},{64,56},{72,6... | collective-permute-start | bytes 49160 | tf_op jit(solution)/shard_map/ppermute | solution.py:26
  22.3 13.0 %all-to-all-start = ((f32[8,1,4,4,2,128]{5,4,3,2,1,0:T(2,128)}), f32[8,1,4,4,2,128]{5,4,3,2,1,0:T(2,128)S(1)}, u32[]{:S(2)}, u32[]{:S(2)}) async-start(f32[8,1,4,4,2,128]{5,4,3,2,1,0:T(2,128)} %broadcast_in_dim.79), calls=%async_computation | async-start | bytes 262144 | tf_op jit(solution)/shard_map/all_to_all | solution.py:111
  35.3 1.5 fusion.69
  36.9 1.2 fusion.70
  41.6 5.1 %all-to-all-done = f32[8,1,4,4,2,128]{5,4,3,2,1,0:T(2,128)S(1)} async-done(((f32[8,1,4,4,2,128]{5,4,3,2,1,0:T(2,128)}), f32[8,1,4,4,2,128]{5,4,3,2,1,0:T(2,128)S(1)}, u32[]{:S(2)}, u32[]{:S(2)}) %all-to-all-start) | async-done | bytes 131104 | tf_op jit(solution)/shard_map/all_to_all | solution.py:111
  48.1 3.2 %subtract_multiply_fusion = (f32[1,4,2,128,128]{3,2,4,1,0:T(2,128)S(1)}, f32[1,4,2,128,128]{3,2,4,1,0:T(2,128)S(1)}, f32[1,4,2,128,128]{3,2,4,1,0:T(2,128)S(1)}) fusion(f32[1,4,2,127,128]{3,2,4,1,0:T(2,128)} %get-tuple-element.85, f32[1,4,2,1,128]{3,2,4,1,0:T(2,128)S(1)} %copy.1165, f32[1,4,2,1,128]{3,2,4,1,0:T(2,128)S(1)} %copy.1164, ...), kind=kLoop, calls=%fused_computation.47 | loop fusion | flops 1835008 | bytes 4325376 | tf_op jit(solution)/shard_map/mul | solution.py:50
  59.0 1.9 %collective-permute-start.2 = (f32[1,1,4,4,2,128]{5,4,3,2,1,0:T(2,128)}, f32[1,1,4,4,2,128]{5,4,3,2,1,0:T(2,128)}, u32[]{:S(2)}, u32[]{:S(2)}) collective-permute-start(f32[1,1,4,4,2,128]{5,4,3,2,1,0:T(2,128)} %get-tuple-element.139), channel_id=1, source_target_pairs={{0,8},{8,16},{16,24},{24,32},{32,40},{40,48},{48,56},{56,64},{64,7... | collective-permute-start | bytes 49160 | tf_op jit(solution)/shard_map/ppermute | solution.py:23
  60.9 10.6 %collective-permute-start.3 = (f32[1,1,4,4,2,128]{5,4,3,2,1,0:T(2,128)}, f32[1,1,4,4,2,128]{5,4,3,2,1,0:T(2,128)}, u32[]{:S(2)}, u32[]{:S(2)}) collective-permute-start(f32[1,1,4,4,2,128]{5,4,3,2,1,0:T(2,128)} %get-tuple-element.139), channel_id=1, source_target_pairs={{8,0},{16,8},{24,16},{32,24},{40,32},{48,40},{56,48},{64,56},{72,6... | collective-permute-start | bytes 49160 | tf_op jit(solution)/shard_map/ppermute | solution.py:26
  77.8 6.9 %all-to-all-start.1 = ((f32[8,1,4,4,2,128]{5,4,3,2,1,0:T(2,128)}), f32[8,1,4,4,2,128]{5,4,3,2,1,0:T(2,128)}, u32[]{:S(2)}, u32[]{:S(2)}) async-start(f32[8,1,4,4,2,128]{5,4,3,2,1,0:T(2,128)} %broadcast_in_dim.144), calls=%async_computation.1 | async-start | bytes 262144 | tf_op jit(solution)/shard_map/all_to_all | solution.py:111
  86.5 1.6 copy.1212
  88.1 1.7 fusion.64
  102.8 1.5 negate_multiply_fusion.9
  106.4 1.3 copy_multiply_fusion.1
  109.8 2.0 %copy_add_fusion.5 = (f32[1,4,2,128,128]{4,3,1,2,0:T(8,128)}, f32[1,4,2,128,128]{4,3,1,2,0:T(8,128)S(1)}) fusion(f32[1,4,2,128,128]{4,3,1,2,0:T(8,128)} %copy.1208, f32[1,4,2,128,128]{4,3,2,1,0:T(8,128)S(1)} %get-tuple-element.27, f32[1,1,2,128,128]{4,3,1,2,0:T(8,128)} %copy-done.13, f32[1,1,2,128,128]{4,3,1,2,0:T(8,128)S(1)} %copy.1296, ...), kind=kLoop, calls=%fused_computation.49 | loop fusion | flops 917504 | bytes 2621440 | tf_op jit(solution)/shard_map/transpose(jvp())/add_any | solution.py:48
  114.8 12.1 %all-to-all-start.2 = ((f32[8,1,4,4,2,128]{5,4,3,2,1,0:T(2,128)}), f32[8,1,4,4,2,128]{5,4,3,2,1,0:T(2,128)S(1)}, u32[]{:S(2)}, u32[]{:S(2)}) async-start(f32[8,1,4,4,2,128]{5,4,3,2,1,0:T(2,128)} %bitcast.54), calls=%async_computation.2 | async-start | bytes 262144 | tf_op jit(solution)/shard_map/all_to_all | solution.py:129
  127.0 2.1 %collective-permute-start.4 = (f32[1,1,4,4,2,128]{5,4,3,2,1,0:T(2,128)S(1)}, f32[1,1,4,4,2,128]{5,4,3,2,1,0:T(2,128)S(1)}, u32[]{:S(2)}, u32[]{:S(2)}) collective-permute-start(f32[1,1,4,4,2,128]{5,4,3,2,1,0:T(2,128)S(1)} %slice.271), channel_id=1, source_target_pairs={{0,8},{8,16},{16,24},{24,32},{32,40},{40,48},{48,56},{56,64},{64,7... | collective-permute-start | bytes 49160 | tf_op jit(solution)/shard_map/ppermute | solution.py:23
  129.1 10.8 %collective-permute-start.5 = (f32[1,1,4,4,2,128]{5,4,3,2,1,0:T(2,128)S(1)}, f32[1,1,4,4,2,128]{5,4,3,2,1,0:T(2,128)S(1)}, u32[]{:S(2)}, u32[]{:S(2)}) collective-permute-start(f32[1,1,4,4,2,128]{5,4,3,2,1,0:T(2,128)S(1)} %slice.273), channel_id=1, source_target_pairs={{8,0},{16,8},{24,16},{32,24},{40,32},{48,40},{56,48},{64,56},{72,6... | collective-permute-start | bytes 49160 | tf_op jit(solution)/shard_map/ppermute | solution.py:26
  143.2 1.4 fusion.7
  147.5 1.8 negate_multiply_fusion.7
  159.4 12.1 %all-to-all-start.3 = ((f32[8,1,4,4,2,128]{5,4,3,2,1,0:T(2,128)}), f32[8,1,4,4,2,128]{5,4,3,2,1,0:T(2,128)S(1)}, u32[]{:S(2)}, u32[]{:S(2)}) async-start(f32[8,1,4,4,2,128]{5,4,3,2,1,0:T(2,128)} %bitcast.72), calls=%async_computation.3 | async-start | bytes 262144 | tf_op jit(solution)/shard_map/all_to_all | solution.py:129
  171.6 1.9 %collective-permute-start.6 = (f32[1,1,4,4,2,128]{5,4,3,2,1,0:T(2,128)S(1)}, f32[1,1,4,4,2,128]{5,4,3,2,1,0:T(2,128)S(1)}, u32[]{:S(2)}, u32[]{:S(2)}) collective-permute-start(f32[1,1,4,4,2,128]{5,4,3,2,1,0:T(2,128)S(1)} %slice.277), channel_id=1, source_target_pairs={{0,8},{8,16},{16,24},{24,32},{32,40},{40,48},{48,56},{56,64},{64,7... | collective-permute-start | bytes 49160 | tf_op jit(solution)/shard_map/ppermute | solution.py:23
  173.6 10.6 %collective-permute-start.7 = (f32[1,1,4,4,2,128]{5,4,3,2,1,0:T(2,128)S(1)}, f32[1,1,4,4,2,128]{5,4,3,2,1,0:T(2,128)S(1)}, u32[]{:S(2)}, u32[]{:S(2)}) collective-permute-start(f32[1,1,4,4,2,128]{5,4,3,2,1,0:T(2,128)S(1)} %slice.279), channel_id=1, source_target_pairs={{8,0},{16,8},{24,16},{32,24},{40,32},{48,40},{56,48},{64,56},{72,6... | collective-permute-start | bytes 49160 | tf_op jit(solution)/shard_map/ppermute | solution.py:26
  (290 shorter events, 62.2 us)
Async XLA Ops:
  4.7 36.9 %collective-permute-start = (f32[1,1,4,4,2,128]{5,4,3,2,1,0:T(2,128)S(1)}, f32[1,1,4,4,2,128]{5,4,3,2,1,0:T(2,128)S(1)}, u32[]{:S(2)}, u32[]{:S(2)}) collective-permute-start(f32[1,1,4,4,2,128]{5,4,3,2,1,0:T(2,128)S(1)} %get-tuple-element.145), channel_id=1, source_target_pairs={{0,8},{8,16},{16,24},{24,32},{32,40},{40,48},{48,56},{56,64},{64,7... | collective-permute-start | bytes 49160 | tf_op jit(solution)/shard_map/ppermute | solution.py:23
  6.6 35.0 %collective-permute-start.1 = (f32[1,1,4,4,2,128]{5,4,3,2,1,0:T(2,128)S(1)}, f32[1,1,4,4,2,128]{5,4,3,2,1,0:T(2,128)S(1)}, u32[]{:S(2)}, u32[]{:S(2)}) collective-permute-start(f32[1,1,4,4,2,128]{5,4,3,2,1,0:T(2,128)S(1)} %get-tuple-element.145), channel_id=1, source_target_pairs={{8,0},{16,8},{24,16},{32,24},{40,32},{48,40},{56,48},{64,56},{72,6... | collective-permute-start | bytes 49160 | tf_op jit(solution)/shard_map/ppermute | solution.py:26
  22.3 24.4 %all-to-all-start = ((f32[8,1,4,4,2,128]{5,4,3,2,1,0:T(2,128)}), f32[8,1,4,4,2,128]{5,4,3,2,1,0:T(2,128)S(1)}, u32[]{:S(2)}, u32[]{:S(2)}) async-start(f32[8,1,4,4,2,128]{5,4,3,2,1,0:T(2,128)} %broadcast_in_dim.79), calls=%async_computation | async-start | bytes 262144 | tf_op jit(solution)/shard_map/all_to_all | solution.py:111
  39.6 7.5 %copy-start.44 = (pred[1,4,1,1,1,1,40]{6,1,5,4,3,2,0:T(4,128)(4,1)}, pred[1,4,1,1,1,1,40]{6,1,5,4,3,2,0:T(4,128)(4,1)S(1)}, u32[]{:S(2)}) copy-start(pred[1,4,1,1,1,1,40]{6,1,5,4,3,2,0:T(4,128)(4,1)S(1)} %fusion.49) | copy-start | bytes 484
  39.6 7.8 %copy-start.42 = (pred[4]{0:T(512)(128)(4,1)}, pred[4]{0:T(512)(128)(4,1)S(1)}, u32[]{:S(2)}) copy-start(pred[4]{0:T(512)(128)(4,1)S(1)} %compare_bitcast_fusion.1) | copy-start | bytes 16
  59.0 38.3 %collective-permute-start.2 = (f32[1,1,4,4,2,128]{5,4,3,2,1,0:T(2,128)}, f32[1,1,4,4,2,128]{5,4,3,2,1,0:T(2,128)}, u32[]{:S(2)}, u32[]{:S(2)}) collective-permute-start(f32[1,1,4,4,2,128]{5,4,3,2,1,0:T(2,128)} %get-tuple-element.139), channel_id=1, source_target_pairs={{0,8},{8,16},{16,24},{24,32},{32,40},{40,48},{48,56},{56,64},{64,7... | collective-permute-start | bytes 49160 | tf_op jit(solution)/shard_map/ppermute | solution.py:23
  60.9 36.4 %collective-permute-start.3 = (f32[1,1,4,4,2,128]{5,4,3,2,1,0:T(2,128)}, f32[1,1,4,4,2,128]{5,4,3,2,1,0:T(2,128)}, u32[]{:S(2)}, u32[]{:S(2)}) collective-permute-start(f32[1,1,4,4,2,128]{5,4,3,2,1,0:T(2,128)} %get-tuple-element.139), channel_id=1, source_target_pairs={{8,0},{16,8},{24,16},{32,24},{40,32},{48,40},{56,48},{64,56},{72,6... | collective-permute-start | bytes 49160 | tf_op jit(solution)/shard_map/ppermute | solution.py:26
  77.8 19.4 %all-to-all-start.1 = ((f32[8,1,4,4,2,128]{5,4,3,2,1,0:T(2,128)}), f32[8,1,4,4,2,128]{5,4,3,2,1,0:T(2,128)}, u32[]{:S(2)}, u32[]{:S(2)}) async-start(f32[8,1,4,4,2,128]{5,4,3,2,1,0:T(2,128)} %broadcast_in_dim.144), calls=%async_computation.1 | async-start | bytes 262144 | tf_op jit(solution)/shard_map/all_to_all | solution.py:111
  88.1 1.7 copy-start.33
  88.1 1.7 copy-start.34
  114.1 25.8 %copy-start.30 = (f32[1,1,2,128,128]{3,2,4,1,0:T(2,128)S(1)}, f32[1,1,2,128,128]{3,2,4,1,0:T(2,128)}, u32[]{:S(2)}) copy-start(f32[1,1,2,128,128]{3,2,4,1,0:T(2,128)} %get-tuple-element.149) | copy-start | bytes 393220
  114.8 25.1 %copy-start.21 = (f32[1,1,2,128,128]{3,2,4,1,0:T(2,128)S(1)}, f32[1,1,2,128,128]{3,2,4,1,0:T(2,128)}, u32[]{:S(2)}) copy-start(f32[1,1,2,128,128]{3,2,4,1,0:T(2,128)} %get-tuple-element.114) | copy-start | bytes 393220
  114.8 25.1 %copy-start.22 = (f32[1,1,2,128,128]{3,2,4,1,0:T(2,128)S(1)}, f32[1,1,2,128,128]{3,2,4,1,0:T(2,128)}, u32[]{:S(2)}) copy-start(f32[1,1,2,128,128]{3,2,4,1,0:T(2,128)} %get-tuple-element.115) | copy-start | bytes 393220
  114.8 27.0 %all-to-all-start.2 = ((f32[8,1,4,4,2,128]{5,4,3,2,1,0:T(2,128)}), f32[8,1,4,4,2,128]{5,4,3,2,1,0:T(2,128)S(1)}, u32[]{:S(2)}, u32[]{:S(2)}) async-start(f32[8,1,4,4,2,128]{5,4,3,2,1,0:T(2,128)} %bitcast.54), calls=%async_computation.2 | async-start | bytes 262144 | tf_op jit(solution)/shard_map/all_to_all | solution.py:129
  127.0 13.0 %copy-start.5 = (f32[1,4,2,127,128]{3,1,2,4,0:T(4,128)S(1)}, f32[1,4,2,127,128]{3,1,2,4,0:T(4,128)}, u32[]{:S(2)}) copy-start(f32[1,4,2,127,128]{3,1,2,4,0:T(4,128)} %split.125) | copy-start | bytes 1560580
  127.0 14.9 %collective-permute-start.4 = (f32[1,1,4,4,2,128]{5,4,3,2,1,0:T(2,128)S(1)}, f32[1,1,4,4,2,128]{5,4,3,2,1,0:T(2,128)S(1)}, u32[]{:S(2)}, u32[]{:S(2)}) collective-permute-start(f32[1,1,4,4,2,128]{5,4,3,2,1,0:T(2,128)S(1)} %slice.271), channel_id=1, source_target_pairs={{0,8},{8,16},{16,24},{24,32},{32,40},{40,48},{48,56},{56,64},{64,7... | collective-permute-start | bytes 49160 | tf_op jit(solution)/shard_map/ppermute | solution.py:23
  129.1 12.8 %collective-permute-start.5 = (f32[1,1,4,4,2,128]{5,4,3,2,1,0:T(2,128)S(1)}, f32[1,1,4,4,2,128]{5,4,3,2,1,0:T(2,128)S(1)}, u32[]{:S(2)}, u32[]{:S(2)}) collective-permute-start(f32[1,1,4,4,2,128]{5,4,3,2,1,0:T(2,128)S(1)} %slice.273), channel_id=1, source_target_pairs={{8,0},{16,8},{24,16},{32,24},{40,32},{48,40},{56,48},{64,56},{72,6... | collective-permute-start | bytes 49160 | tf_op jit(solution)/shard_map/ppermute | solution.py:26
  141.9 1.3 copy-start.4
  146.3 1.2 copy-start.3
  158.6 25.5 %copy-start.19 = (f32[1,1,4,128,128]{4,3,2,1,0:T(8,128)S(1)}, f32[1,1,4,128,128]{4,3,2,1,0:T(8,128)}, u32[]{:S(2)}) copy-start(f32[1,1,4,128,128]{4,3,2,1,0:T(8,128)} %get-tuple-element.43) | copy-start | bytes 786436
  159.4 24.7 %copy-start.18 = (f32[1,1,4,128,128]{4,3,2,1,0:T(8,128)S(1)}, f32[1,1,4,128,128]{4,3,2,1,0:T(8,128)}, u32[]{:S(2)}) copy-start(f32[1,1,4,128,128]{4,3,2,1,0:T(8,128)} %get-tuple-element.45) | copy-start | bytes 786436
  159.4 25.6 %all-to-all-start.3 = ((f32[8,1,4,4,2,128]{5,4,3,2,1,0:T(2,128)}), f32[8,1,4,4,2,128]{5,4,3,2,1,0:T(2,128)S(1)}, u32[]{:S(2)}, u32[]{:S(2)}) async-start(f32[8,1,4,4,2,128]{5,4,3,2,1,0:T(2,128)} %bitcast.72), calls=%async_computation.3 | async-start | bytes 262144 | tf_op jit(solution)/shard_map/all_to_all | solution.py:129
  171.6 13.4 %collective-permute-start.6 = (f32[1,1,4,4,2,128]{5,4,3,2,1,0:T(2,128)S(1)}, f32[1,1,4,4,2,128]{5,4,3,2,1,0:T(2,128)S(1)}, u32[]{:S(2)}, u32[]{:S(2)}) collective-permute-start(f32[1,1,4,4,2,128]{5,4,3,2,1,0:T(2,128)S(1)} %slice.277), channel_id=1, source_target_pairs={{0,8},{8,16},{16,24},{24,32},{32,40},{40,48},{48,56},{56,64},{64,7... | collective-permute-start | bytes 49160 | tf_op jit(solution)/shard_map/ppermute | solution.py:23
  173.6 12.0 %collective-permute-start.7 = (f32[1,1,4,4,2,128]{5,4,3,2,1,0:T(2,128)S(1)}, f32[1,1,4,4,2,128]{5,4,3,2,1,0:T(2,128)S(1)}, u32[]{:S(2)}, u32[]{:S(2)}) collective-permute-start(f32[1,1,4,4,2,128]{5,4,3,2,1,0:T(2,128)S(1)} %slice.279), channel_id=1, source_target_pairs={{8,0},{16,8},{24,16},{32,24},{40,32},{48,40},{56,48},{64,56},{72,6... | collective-permute-start | bytes 49160 | tf_op jit(solution)/shard_map/ppermute | solution.py:26
  (40 other events, 37.4 us)

commit v3 on v2

--- a/solution.py
+++ b/solution.py
@@ -17,13 +17,22 @@
 def with_halo(block, sides, width):
     for axis, dim in sides:
         count = lax.axis_size(axis)
-        forward = [(i, i + 1) for i in range(count - 1)]
-        forward.append((count - 1, 0))
-        backward = [(target, source) for source, target in forward]
-        low = lax.ppermute(
-            lax.slice_in_dim(block, block.shape[dim] - width, None, axis=dim), axis, forward
-        )
-        high = lax.ppermute(lax.slice_in_dim(block, 0, width, axis=dim), axis, backward)
+        up_part = lax.slice_in_dim(block, block.shape[dim] - width, None, axis=dim)
+        down_part = lax.slice_in_dim(block, 0, width, axis=dim)
+        if count % 2 == 0:
+            even = lax.axis_index(axis) % 2 == 0
+            pairs_near = [(i, i ^ 1) for i in range(count)]
+            pairs_far = [(i, (i + 1) % count if i % 2 else (i - 1) % count) for i in range(count)]
+            near = lax.ppermute(jnp.where(even, up_part, down_part), axis, pairs_near)
+            far = lax.ppermute(jnp.where(even, down_part, up_part), axis, pairs_far)
+            low = jnp.where(even, far, near)
+            high = jnp.where(even, near, far)
+        else:
+            forward = [(i, i + 1) for i in range(count - 1)]
+            forward.append((count - 1, 0))
+            backward = [(target, source) for source, target in forward]
+            low = lax.ppermute(up_part, axis, forward)
+            high = lax.ppermute(down_part, axis, backward)
         block = jnp.concatenate([low, block, high], axis=dim)
     return block
 

time: 189 us -> 181 us (0.958)
  the two profiles are of different devices: /device:TPU:2 before, /device:TPU:1 now
where the time goes in v3:
time: 181 us; the launch traced here: 179 us
  starting transfers between devices  78 us (43%)
  local copies, waits for them, and re-layouts  47.9 us (26%)
  other arithmetic  37 us (20%)
  waiting for transfers between devices  12.8 us (7%)
  between operations  2.19 us (1%)
    ppermute x4, starting transfers between devices, with_halo(): near = lax.ppermute(jnp.where(even, up_part, down_part), axis, pairs_near)  32.5 us
    all_to_all x2, starting transfers between devices, fill_back(): returned = lax.all_to_all(ct_cands[:group_size], 'tile', 0, 0, tiled=True)  18.2 us
    all_to_all x2, starting transfers between devices, gather_rims(): grouped = lax.all_to_all(copies, 'tile', 0, 0, tiled=True)  15.9 us
    unnamed x92, local copies, waits for them, and re-layouts  15.3 us
    all_to_all x2, waiting for transfers between devices, gather_rims(): grouped = lax.all_to_all(copies, 'tile', 0, 0, tiled=True)  12.7 us
    ppermute x4, starting transfers between devices, with_halo(): far = lax.ppermute(jnp.where(even, down_part, up_part), axis, pairs_far)  11.4 us
    mul x3, other arithmetic, step_tiles(): grad_x = 0.5 * (east - west)  5.95 us
    slice x5, local copies, waits for them, and re-layouts, fill_back(): returned = lax.all_to_all(ct_cands[:group_size], 'tile', 0, 0, tiled=True)  3.84 us
  transfers between devices with their start and end apart: 12, of which 2 were waited for; matrix products, arithmetic and copies ran while one was open for 15% of the time, Pallas kernels for 0%

profile of v3, /device:TPU:1, one launch (start us, length us, event | category | flops | bytes accessed | tf_op | source)
XLA Modules:
  0.0 178.8 jit_solution(7040007399626113626)
XLA Ops:
  2.3 1.5 copy_multiply_fusion.1
  4.8 4.6 %collective-permute-start = (f32[1,1,4,4,2,128]{5,4,3,2,1,0:T(2,128)S(1)}, f32[1,1,4,4,2,128]{5,4,3,2,1,0:T(2,128)S(1)}, u32[]{:S(2)}, u32[]{:S(2)}) collective-permute-start(f32[1,1,4,4,2,128]{5,4,3,2,1,0:T(2,128)S(1)} %get-tuple-element.161), channel_id=1, source_target_pairs={{0,760},{8,16},{16,8},{24,32},{32,24},{40,48},{48,40},{56,64},{64,... | collective-permute-start | bytes 49160 | tf_op jit(solution)/shard_map/ppermute | solution.py:27
  9.4 13.9 %collective-permute-start.1 = (f32[1,1,4,4,2,128]{5,4,3,2,1,0:T(2,128)S(1)}, f32[1,1,4,4,2,128]{5,4,3,2,1,0:T(2,128)S(1)}, u32[]{:S(2)}, u32[]{:S(2)}) collective-permute-start(f32[1,1,4,4,2,128]{5,4,3,2,1,0:T(2,128)S(1)} %get-tuple-element.161), channel_id=1, source_target_pairs={{0,8},{8,0},{16,24},{24,16},{32,40},{40,32},{48,56},{56,48},{64,72... | collective-permute-start | bytes 49160 | tf_op jit(solution)/shard_map/ppermute | solution.py:26
  24.0 11.6 %all-to-all-start = ((f32[8,1,4,4,2,128]{5,4,3,2,1,0:T(2,128)}), f32[8,1,4,4,2,128]{5,4,3,2,1,0:T(2,128)S(1)}, u32[]{:S(2)}, u32[]{:S(2)}) async-start(f32[8,1,4,4,2,128]{5,4,3,2,1,0:T(2,128)} %broadcast_in_dim.79), calls=%async_computation | async-start | bytes 262144 | tf_op jit(solution)/shard_map/all_to_all | solution.py:120
  35.5 1.5 fusion.72
  39.8 7.6 %all-to-all-done = f32[8,1,4,4,2,128]{5,4,3,2,1,0:T(2,128)S(1)} async-done(((f32[8,1,4,4,2,128]{5,4,3,2,1,0:T(2,128)}), f32[8,1,4,4,2,128]{5,4,3,2,1,0:T(2,128)S(1)}, u32[]{:S(2)}, u32[]{:S(2)}) %all-to-all-start) | async-done | bytes 131104 | tf_op jit(solution)/shard_map/all_to_all | solution.py:120
  49.2 3.3 %subtract_multiply_fusion.1 = (f32[1,4,2,128,128]{4,2,3,1,0:T(2,128)S(1)}, f32[1,4,2,128,128]{4,2,3,1,0:T(2,128)S(1)}, f32[1,4,2,128,128]{4,2,3,1,0:T(2,128)S(1)}) fusion(f32[1,4,2,128,127]{4,2,3,1,0:T(2,128)} %get-tuple-element.93, f32[1,4,2,128,1]{4,2,3,1,0:T(2,128)S(1)} %copy.1933, f32[1,4,2,128,1]{4,2,3,1,0:T(2,128)S(1)} %copy.1932, ...), kind=kLoop, calls=%fused_computation.55 | loop fusion | flops 1835008 | bytes 4325376 | tf_op jit(solution)/shard_map/mul | solution.py:58
  58.5 1.9 %collective-permute-start.2 = (f32[1,1,4,4,2,128]{5,4,3,2,1,0:T(2,128)}, f32[1,1,4,4,2,128]{5,4,3,2,1,0:T(2,128)}, u32[]{:S(2)}, u32[]{:S(2)}) collective-permute-start(f32[1,1,4,4,2,128]{5,4,3,2,1,0:T(2,128)} %get-tuple-element.155), channel_id=1, source_target_pairs={{0,760},{8,16},{16,8},{24,32},{32,24},{40,48},{48,40},{56,64},{64,... | collective-permute-start | bytes 49160 | tf_op jit(solution)/shard_map/ppermute | solution.py:27
  60.4 3.4 %collective-permute-start.3 = (f32[1,1,4,4,2,128]{5,4,3,2,1,0:T(2,128)}, f32[1,1,4,4,2,128]{5,4,3,2,1,0:T(2,128)}, u32[]{:S(2)}, u32[]{:S(2)}) collective-permute-start(f32[1,1,4,4,2,128]{5,4,3,2,1,0:T(2,128)} %get-tuple-element.155), channel_id=1, source_target_pairs={{0,8},{8,0},{16,24},{24,16},{32,40},{40,32},{48,56},{56,48},{64,72... | collective-permute-start | bytes 49160 | tf_op jit(solution)/shard_map/ppermute | solution.py:26
  71.6 4.3 %all-to-all-start.1 = ((f32[8,1,4,4,2,128]{5,4,3,2,1,0:T(2,128)}), f32[8,1,4,4,2,128]{5,4,3,2,1,0:T(2,128)}, u32[]{:S(2)}, u32[]{:S(2)}) async-start(f32[8,1,4,4,2,128]{5,4,3,2,1,0:T(2,128)} %broadcast_in_dim.144), calls=%async_computation.1 | async-start | bytes 262144 | tf_op jit(solution)/shard_map/all_to_all | solution.py:120
  82.5 5.1 %all-to-all-done.1 = f32[8,1,4,4,2,128]{5,4,3,2,1,0:T(2,128)} async-done(((f32[8,1,4,4,2,128]{5,4,3,2,1,0:T(2,128)}), f32[8,1,4,4,2,128]{5,4,3,2,1,0:T(2,128)}, u32[]{:S(2)}, u32[]{:S(2)}) %all-to-all-start.1) | async-done | bytes 131104 | tf_op jit(solution)/shard_map/all_to_all | solution.py:120
  91.9 2.3 %fusion.1 = f32[1,4,2,128,128]{4,2,3,1,0:T(2,128)S(1)} fusion(f32[1,4,2,128,1]{4,2,3,1,0:T(2,128)S(1)} %copy.1959, f32[1,4,2,128,127]{4,2,3,1,0:T(2,128)S(1)} %copy.2057, f32[1,4,2,128,127]{4,2,3,1,0:T(2,128)S(1)} %copy.2058, f32[1,4,2,128,1]{4,2,3,1,0:T(2,128)} %copy.1961), kind=kLoop, calls=%fused_computation.9 | loop fusion | flops 524288 | bytes 1572864 | tf_op jit(solution)/shard_map/jvp()/mul | solution.py:58
  95.3 1.9 %fusion.20 = (f32[1,1,2,128,128]{4,2,3,1,0:T(2,128)}, f32[1,1,2,128,128]{4,2,3,1,0:T(2,128)}, f32[1,1,2,128,128]{4,2,3,1,0:T(2,128)S(1)}, f32[1,1,2,128,128]{4,2...) fusion(f32[1,4,2,128,128]{4,2,3,1,0:T(2,128)S(1)} %fusion, ...), kind=kLoop, calls=%fused_computation.73 | loop fusion | flops 983040 | bytes 2883584 | tf_op jit(solution)/shard_map/transpose(jvp())/add_any | solution.py:67
  106.5 1.7 slice.261
  108.1 6.0 %all-to-all-start.2 = ((f32[8,1,4,4,2,128]{5,4,3,2,1,0:T(2,128)}), f32[8,1,4,4,2,128]{5,4,3,2,1,0:T(2,128)}, u32[]{:S(2)}, u32[]{:S(2)}) async-start(f32[8,1,4,4,2,128]{5,4,3,2,1,0:T(2,128)} %bitcast.209), calls=%async_computation.2 | async-start | bytes 262144 | tf_op jit(solution)/shard_map/all_to_all | solution.py:138
  114.7 1.9 %split.125 = f32[1,4,2,127,128]{4,2,3,1,0:T(2,128)} slice(f32[1,4,2,128,128]{4,2,3,1,0:T(2,128)} %get-tuple-element.36), slice={[0:1], [0:4], [0:2], [1:128], [0:128]} | slice | bytes 1040384 | tf_op jit(solution)/shard_map/transpose(jvp())/split | solution.py:56
  118.3 3.0 %collective-permute-start.4 = (f32[1,1,4,4,2,128]{5,4,3,2,1,0:T(2,128)S(1)}, f32[1,1,4,4,2,128]{5,4,3,2,1,0:T(2,128)S(1)}, u32[]{:S(2)}, u32[]{:S(2)}) collective-permute-start(f32[1,1,4,4,2,128]{5,4,3,2,1,0:T(2,128)S(1)} %select_n.203), channel_id=1, source_target_pairs={{0,760},{8,16},{16,8},{24,32},{32,24},{40,48},{48,40},{56,64},{64,... | collective-permute-start | bytes 49160 | tf_op jit(solution)/shard_map/ppermute | solution.py:27
  121.4 9.7 %collective-permute-start.5 = (f32[1,1,4,4,2,128]{5,4,3,2,1,0:T(2,128)S(1)}, f32[1,1,4,4,2,128]{5,4,3,2,1,0:T(2,128)S(1)}, u32[]{:S(2)}, u32[]{:S(2)}) collective-permute-start(f32[1,1,4,4,2,128]{5,4,3,2,1,0:T(2,128)S(1)} %select_n.205), channel_id=1, source_target_pairs={{0,8},{8,0},{16,24},{24,16},{32,40},{40,32},{48,56},{56,48},{64,72... | collective-permute-start | bytes 49160 | tf_op jit(solution)/shard_map/ppermute | solution.py:26
  131.1 2.6 %pad_add_fusion.8 = f32[1,4,2,128,128]{4,2,3,1,0:T(2,128)} fusion(f32[1,4,2,127,128]{4,2,3,1,0:T(2,128)} %split.125, f32[1,1,2,128,128]{4,2,3,1,0:T(2,128)} %get-tuple-element.165, f32[1,1,2,128,128]{4,2,3,1,0:T(2,128)} %get-tuple-element.164, f32[1,1,2,128,128]{4,2,3,1,0:T(2,128)S(1)} %copy-done.22, f32[1,1,2,128,128]{4,2,3,1,0:T(2,128)S(1)} %copy-done.21, ...), kind=kLoop, calls=%fused_computation.49 | loop fusion | flops 917504 | bytes 2093056 | tf_op jit(solution)/shard_map/transpose(jvp())/add_any | solution.py:56
  136.8 1.7 fusion.12
  140.1 1.8 multiply_add_fusion.1
  150.8 12.2 %all-to-all-start.3 = ((f32[8,1,4,4,2,128]{5,4,3,2,1,0:T(2,128)}), f32[8,1,4,4,2,128]{5,4,3,2,1,0:T(2,128)S(1)}, u32[]{:S(2)}, u32[]{:S(2)}) async-start(f32[8,1,4,4,2,128]{5,4,3,2,1,0:T(2,128)} %bitcast.74), calls=%async_computation.3 | async-start | bytes 262144 | tf_op jit(solution)/shard_map/all_to_all | solution.py:138
  163.6 1.9 %collective-permute-start.6 = (f32[1,1,4,4,2,128]{5,4,3,2,1,0:T(2,128)}, f32[1,1,4,4,2,128]{5,4,3,2,1,0:T(2,128)}, u32[]{:S(2)}, u32[]{:S(2)}) collective-permute-start(f32[1,1,4,4,2,128]{5,4,3,2,1,0:T(2,128)} %select_n.211), channel_id=1, source_target_pairs={{0,760},{8,16},{16,8},{24,32},{32,24},{40,48},{48,40},{56,64},{64,... | collective-permute-start | bytes 49160 | tf_op jit(solution)/shard_map/ppermute | solution.py:27
  166.1 5.6 %collective-permute-start.7 = (f32[1,1,4,4,2,128]{5,4,3,2,1,0:T(2,128)}, f32[1,1,4,4,2,128]{5,4,3,2,1,0:T(2,128)S(1)}, u32[]{:S(2)}, u32[]{:S(2)}) collective-permute-start(f32[1,1,4,4,2,128]{5,4,3,2,1,0:T(2,128)} %select_n.213), channel_id=1, source_target_pairs={{0,8},{8,0},{16,24},{24,16},{32,40},{40,32},{48,56},{56,48},{64,72... | collective-permute-start | bytes 49160 | tf_op jit(solution)/shard_map/ppermute | solution.py:26
  (243 shorter events, 65.8 us)
Async XLA Ops:
  4.8 35.0 %collective-permute-start = (f32[1,1,4,4,2,128]{5,4,3,2,1,0:T(2,128)S(1)}, f32[1,1,4,4,2,128]{5,4,3,2,1,0:T(2,128)S(1)}, u32[]{:S(2)}, u32[]{:S(2)}) collective-permute-start(f32[1,1,4,4,2,128]{5,4,3,2,1,0:T(2,128)S(1)} %get-tuple-element.161), channel_id=1, source_target_pairs={{0,760},{8,16},{16,8},{24,32},{32,24},{40,48},{48,40},{56,64},{64,... | collective-permute-start | bytes 49160 | tf_op jit(solution)/shard_map/ppermute | solution.py:27
  9.4 30.4 %collective-permute-start.1 = (f32[1,1,4,4,2,128]{5,4,3,2,1,0:T(2,128)S(1)}, f32[1,1,4,4,2,128]{5,4,3,2,1,0:T(2,128)S(1)}, u32[]{:S(2)}, u32[]{:S(2)}) collective-permute-start(f32[1,1,4,4,2,128]{5,4,3,2,1,0:T(2,128)S(1)} %get-tuple-element.161), channel_id=1, source_target_pairs={{0,8},{8,0},{16,24},{24,16},{32,40},{40,32},{48,56},{56,48},{64,72... | collective-permute-start | bytes 49160 | tf_op jit(solution)/shard_map/ppermute | solution.py:26
  24.0 23.4 %all-to-all-start = ((f32[8,1,4,4,2,128]{5,4,3,2,1,0:T(2,128)}), f32[8,1,4,4,2,128]{5,4,3,2,1,0:T(2,128)S(1)}, u32[]{:S(2)}, u32[]{:S(2)}) async-start(f32[8,1,4,4,2,128]{5,4,3,2,1,0:T(2,128)} %broadcast_in_dim.79), calls=%async_computation | async-start | bytes 262144 | tf_op jit(solution)/shard_map/all_to_all | solution.py:120
  39.7 49.2 %copy-start.33 = (pred[1,4,1,1,1,1,40]{6,1,5,4,3,2,0:T(4,128)(4,1)}, pred[1,4,1,1,1,1,40]{6,1,5,4,3,2,0:T(4,128)(4,1)S(1)}, u32[]{:S(2)}) copy-start(pred[1,4,1,1,1,1,40]{6,1,5,4,3,2,0:T(4,128)(4,1)S(1)} %fusion.54) | copy-start | bytes 484
  39.8 65.0 %copy-start.31 = (pred[4]{0:T(512)(128)(4,1)}, pred[4]{0:T(512)(128)(4,1)S(1)}, u32[]{:S(2)}) copy-start(pred[4]{0:T(512)(128)(4,1)S(1)} %compare_bitcast_fusion.1) | copy-start | bytes 16
  58.5 23.2 %collective-permute-start.2 = (f32[1,1,4,4,2,128]{5,4,3,2,1,0:T(2,128)}, f32[1,1,4,4,2,128]{5,4,3,2,1,0:T(2,128)}, u32[]{:S(2)}, u32[]{:S(2)}) collective-permute-start(f32[1,1,4,4,2,128]{5,4,3,2,1,0:T(2,128)} %get-tuple-element.155), channel_id=1, source_target_pairs={{0,760},{8,16},{16,8},{24,32},{32,24},{40,48},{48,40},{56,64},{64,... | collective-permute-start | bytes 49160 | tf_op jit(solution)/shard_map/ppermute | solution.py:27
  60.4 21.3 %collective-permute-start.3 = (f32[1,1,4,4,2,128]{5,4,3,2,1,0:T(2,128)}, f32[1,1,4,4,2,128]{5,4,3,2,1,0:T(2,128)}, u32[]{:S(2)}, u32[]{:S(2)}) collective-permute-start(f32[1,1,4,4,2,128]{5,4,3,2,1,0:T(2,128)} %get-tuple-element.155), channel_id=1, source_target_pairs={{0,8},{8,0},{16,24},{24,16},{32,40},{40,32},{48,56},{56,48},{64,72... | collective-permute-start | bytes 49160 | tf_op jit(solution)/shard_map/ppermute | solution.py:26
  70.9 5.0 %copy-start.28 = (f32[1,1,128,128]{3,1,2,0:T(1,128)S(1)}, f32[1,1,128,128]{3,1,2,0:T(1,128)}, u32[]{:S(2)}) copy-start(f32[1,1,128,128]{3,1,2,0:T(1,128)} %get-tuple-element.131) | copy-start | bytes 196612
  70.9 5.0 %copy-start.29 = (f32[1,1,128,128]{3,1,2,0:T(1,128)S(1)}, f32[1,1,128,128]{3,1,2,0:T(1,128)}, u32[]{:S(2)}) copy-start(f32[1,1,128,128]{3,1,2,0:T(1,128)} %get-tuple-element.132) | copy-start | bytes 196612
  71.6 4.3 %copy-start.12 = (f32[1,2,128,128]{3,2,1,0:T(8,128)S(1)}, f32[1,2,128,128]{3,2,1,0:T(8,128)}, u32[]{:S(2)}) copy-start(f32[1,2,128,128]{3,2,1,0:T(8,128)} %copy-done.11) | copy-start | bytes 393220
  71.6 4.4 %copy-start.26 = (f32[1,1,128,128]{3,1,2,0:T(1,128)S(1)}, f32[1,1,128,128]{3,1,2,0:T(1,128)}, u32[]{:S(2)}) copy-start(f32[1,1,128,128]{3,1,2,0:T(1,128)} %get-tuple-element.129) | copy-start | bytes 196612
  71.6 4.4 %copy-start.27 = (f32[1,1,128,128]{3,1,2,0:T(1,128)S(1)}, f32[1,1,128,128]{3,1,2,0:T(1,128)}, u32[]{:S(2)}) copy-start(f32[1,1,128,128]{3,1,2,0:T(1,128)} %get-tuple-element.130) | copy-start | bytes 196612
  71.6 16.0 %all-to-all-start.1 = ((f32[8,1,4,4,2,128]{5,4,3,2,1,0:T(2,128)}), f32[8,1,4,4,2,128]{5,4,3,2,1,0:T(2,128)}, u32[]{:S(2)}, u32[]{:S(2)}) async-start(f32[8,1,4,4,2,128]{5,4,3,2,1,0:T(2,128)} %broadcast_in_dim.144), calls=%async_computation.1 | async-start | bytes 262144 | tf_op jit(solution)/shard_map/all_to_all | solution.py:120
  91.9 2.3 %copy-start.7 = (f32[1,4,2,127,128]{4,2,3,1,0:T(2,128)S(1)}, f32[1,4,2,127,128]{4,2,3,1,0:T(2,128)}, u32[]{:S(2)}) copy-start(f32[1,4,2,127,128]{4,2,3,1,0:T(2,128)} %copy.2055) | copy-start | bytes 1560580
  91.9 2.3 %copy-start.9 = (f32[1,4,2,127,128]{4,2,3,1,0:T(2,128)S(1)}, f32[1,4,2,127,128]{4,2,3,1,0:T(2,128)}, u32[]{:S(2)}) copy-start(f32[1,4,2,127,128]{4,2,3,1,0:T(2,128)} %copy.2056) | copy-start | bytes 1560580
  108.1 25.6 %all-to-all-start.2 = ((f32[8,1,4,4,2,128]{5,4,3,2,1,0:T(2,128)}), f32[8,1,4,4,2,128]{5,4,3,2,1,0:T(2,128)}, u32[]{:S(2)}, u32[]{:S(2)}) async-start(f32[8,1,4,4,2,128]{5,4,3,2,1,0:T(2,128)} %bitcast.209), calls=%async_computation.2 | async-start | bytes 262144 | tf_op jit(solution)/shard_map/all_to_all | solution.py:138
  116.6 14.5 %copy-start.21 = (f32[1,1,2,128,128]{4,2,3,1,0:T(2,128)S(1)}, f32[1,1,2,128,128]{4,2,3,1,0:T(2,128)}, u32[]{:S(2)}) copy-start(f32[1,1,2,128,128]{4,2,3,1,0:T(2,128)} %get-tuple-element.70) | copy-start | bytes 393220
  116.6 14.5 %copy-start.22 = (f32[1,1,2,128,128]{4,2,3,1,0:T(2,128)S(1)}, f32[1,1,2,128,128]{4,2,3,1,0:T(2,128)}, u32[]{:S(2)}) copy-start(f32[1,1,2,128,128]{4,2,3,1,0:T(2,128)} %get-tuple-element.71) | copy-start | bytes 393220
  118.3 16.3 %collective-permute-start.4 = (f32[1,1,4,4,2,128]{5,4,3,2,1,0:T(2,128)S(1)}, f32[1,1,4,4,2,128]{5,4,3,2,1,0:T(2,128)S(1)}, u32[]{:S(2)}, u32[]{:S(2)}) collective-permute-start(f32[1,1,4,4,2,128]{5,4,3,2,1,0:T(2,128)S(1)} %select_n.203), channel_id=1, source_target_pairs={{0,760},{8,16},{16,8},{24,32},{32,24},{40,48},{48,40},{56,64},{64,... | collective-permute-start | bytes 49160 | tf_op jit(solution)/shard_map/ppermute | solution.py:27
  121.4 13.3 %collective-permute-start.5 = (f32[1,1,4,4,2,128]{5,4,3,2,1,0:T(2,128)S(1)}, f32[1,1,4,4,2,128]{5,4,3,2,1,0:T(2,128)S(1)}, u32[]{:S(2)}, u32[]{:S(2)}) collective-permute-start(f32[1,1,4,4,2,128]{5,4,3,2,1,0:T(2,128)S(1)} %select_n.205), channel_id=1, source_target_pairs={{0,8},{8,0},{16,24},{24,16},{32,40},{40,32},{48,56},{56,48},{64,72... | collective-permute-start | bytes 49160 | tf_op jit(solution)/shard_map/ppermute | solution.py:26
  150.8 12.2 %copy-start.30 = (f32[4,1024]{1,0:T(4,128)S(1)}, f32[4,1024]{1,0:T(4,128)}, u32[]{:S(2)}) copy-start(f32[4,1024]{1,0:T(4,128)} %get-tuple-element.104) | copy-start | bytes 49156
  150.8 25.5 %all-to-all-start.3 = ((f32[8,1,4,4,2,128]{5,4,3,2,1,0:T(2,128)}), f32[8,1,4,4,2,128]{5,4,3,2,1,0:T(2,128)S(1)}, u32[]{:S(2)}, u32[]{:S(2)}) async-start(f32[8,1,4,4,2,128]{5,4,3,2,1,0:T(2,128)} %bitcast.74), calls=%async_computation.3 | async-start | bytes 262144 | tf_op jit(solution)/shard_map/all_to_all | solution.py:138
  163.6 12.7 %collective-permute-start.6 = (f32[1,1,4,4,2,128]{5,4,3,2,1,0:T(2,128)}, f32[1,1,4,4,2,128]{5,4,3,2,1,0:T(2,128)}, u32[]{:S(2)}, u32[]{:S(2)}) collective-permute-start(f32[1,1,4,4,2,128]{5,4,3,2,1,0:T(2,128)} %select_n.211), channel_id=1, source_target_pairs={{0,760},{8,16},{16,8},{24,32},{32,24},{40,48},{48,40},{56,64},{64,... | collective-permute-start | bytes 49160 | tf_op jit(solution)/shard_map/ppermute | solution.py:27
  166.1 10.2 %collective-permute-start.7 = (f32[1,1,4,4,2,128]{5,4,3,2,1,0:T(2,128)}, f32[1,1,4,4,2,128]{5,4,3,2,1,0:T(2,128)S(1)}, u32[]{:S(2)}, u32[]{:S(2)}) collective-permute-start(f32[1,1,4,4,2,128]{5,4,3,2,1,0:T(2,128)} %select_n.213), channel_id=1, source_target_pairs={{0,8},{8,0},{16,24},{24,16},{32,40},{40,32},{48,56},{56,48},{64,72... | collective-permute-start | bytes 49160 | tf_op jit(solution)/shard_map/ppermute | solution.py:26
  (31 other events, 30.1 us)
